TPU v7x, 256 devices: a whole 4x4x8 slice. The times are simulated.
256 devices in a mesh: rep: 8 (over x, core), seq: 32 (over y, z).
Axes of the slice: x: 4, y: 4, z: 8, core: 2. Of those that a mesh axis runs over, the one named last changes fastest.
Arguments:
- tokens: bfloat16 [16, 256, 32, 1024], P('rep', 'seq'), may hold values from -250 to 250
- cotangent: bfloat16 [16, 256, 32, 1024], P('rep', 'seq'), may hold values from -6 to 6
- clip_counts: int32 [8], P('rep'), may hold values from 1 to 2, as said below
- windows: int32 [16, 4, 3], P('rep'), may hold values from 0 to 3, as said below
- window_counts: int32 [16, 4], P('rep'), may hold values from 1 to 3, as said below
- norm_gain: float32 [1024], replicated, may hold values from 0.5 to 4
- norm_bias: float32 [1024], replicated, may hold values from -3 to 3
- qkv_weight: bfloat16 [1024, 3072], replicated, may hold values from -0.5 to 0.5
- out_weight: bfloat16 [1024, 1024], replicated, may hold values from -0.1875 to 0.1875
Outputs:
- grad_input: bfloat16 [16, 256, 32, 1024], P('rep', 'seq')
- grad_qkv_weight: float32 [1024, 3072], P('seq')
- grad_out_weight: float32 [1024, 1024], P('seq')
- grad_gain: float32 [1024], P('seq')
- grad_bias: float32 [1024], P('seq')
Inputs may be any that keep to these rules, and one draw needn't show every extreme that they name: `clip_counts`: slots of a group at or past its count hold no clip; some group is full. `windows`: the first entry of each list is the window itself; the entries of a list are distinct. `window_counts`: some window of every clip uses all 3 entries.
All inputs are finite; a program needn't handle non-finite values.
Results may differ from a plain program's by a relative error of at most 0.025.
The roundings to bfloat16 on the way count: a program that leaves them out, or rounds other values in their place, can miss the bound.
Values may be sent and summed in bfloat16 or wider, within the bound.
No kernel may reach another device: no remote copies, remote signals or barrier semaphores. Data moves between devices by JAX's collectives and lax.ppermute only.
A program may use at most 128 MiB of HBM per device.

v0:
```python
from functools import partial
import math

import jax
import jax.numpy as jnp
from jax import lax
from jax.sharding import PartitionSpec as P

D = 1024
HEADS = 16
HEAD_DIM = 64
WIN = 64
MAXW = 3
NWIN = 4


EPSILON = 1e-05


def frame_mask(window_list, list_count, frame_count):
    used_slot = jnp.arange(MAXW)[None, :] < list_count[:, None]
    listed = (window_list[:, :, None] == jnp.arange(NWIN)[None, None, :]) & used_slot[:, :, None]
    allowed = jnp.any(listed, axis=1).astype(jnp.float32)
    member = (jnp.arange(frame_count)[:, None] // WIN == jnp.arange(NWIN)[None, :]).astype(
        jnp.float32
    )
    return jnp.dot(jnp.dot(member, allowed), member.T) > 0.5


def contract_rows(left_side, right_side):
    return lax.dot_general(
        left_side, right_side, (((0,), (0,)), ((), ())), preferred_element_type=jnp.float32
    )


def times_transpose(left_side, right_side):
    return lax.dot_general(
        left_side, right_side, (((1,), (1,)), ((), ())), preferred_element_type=jnp.float32
    )


def local(
    tokens,
    cotangent,
    clip_counts,
    windows,
    window_counts,
    norm_gain,
    norm_bias,
    qkv_weight,
    out_weight,
):
    seq_size = lax.axis_size("seq")
    rep_size = lax.axis_size("rep")
    clip_count = tokens.shape[0]
    live_slot = jnp.arange(clip_count) < clip_counts[0]
    grad_live = jnp.where(live_slot[:, None, None, None], cotangent, jnp.zeros_like(cotangent))
    gathered, grad_whole = (
        lax.all_to_all(tokens, "seq", split_axis=2, concat_axis=1, tiled=True),
        lax.all_to_all(grad_live, "seq", split_axis=2, concat_axis=1, tiled=True),
    )
    frame_count = gathered.shape[1]
    patch_count = gathered.shape[2]
    row_count = clip_count * frame_count * patch_count
    grad_scale = 1.0 / math.sqrt(clip_count * rep_size * frame_count * patch_count * seq_size)
    factor = HEAD_DIM ** (-0.5)
    head_shape = (clip_count, frame_count, patch_count, HEADS, HEAD_DIM)
    allowed = jax.vmap(partial(frame_mask, frame_count=frame_count))(windows, window_counts)[
        :, None, None
    ]
    flat_input = gathered.reshape(row_count, D).astype(jnp.float32)
    centred = flat_input - jnp.mean(flat_input, axis=1, keepdims=True)
    inv_std = lax.rsqrt(jnp.mean(centred * centred, axis=1, keepdims=True) + EPSILON)
    normal_hat = centred * inv_std
    normed = (normal_hat * norm_gain + norm_bias).astype(jnp.bfloat16)
    projected = jnp.dot(normed, qkv_weight, preferred_element_type=jnp.float32).astype(jnp.bfloat16)
    query_heads = projected[:, :D].reshape(head_shape)
    key_heads = projected[:, D : 2 * D].reshape(head_shape)
    value_heads = projected[:, 2 * D :].reshape(head_shape)
    scores = (
        jnp.einsum("cfphd,cgphd->cphfg", query_heads, key_heads, preferred_element_type=jnp.float32)
        * factor
    )
    row_max = jnp.max(jnp.where(allowed, scores, -1e30), axis=-1, keepdims=True)
    exp_scores = jnp.where(allowed, jnp.exp(scores - row_max), 0.0)
    attn_prob = exp_scores / jnp.sum(exp_scores, axis=-1, keepdims=True)
    prob_bf = attn_prob.astype(jnp.bfloat16)
    attended = jnp.einsum(
        "cphfg,cgphd->cfphd", prob_bf, value_heads, preferred_element_type=jnp.float32
    ).astype(jnp.bfloat16)
    attn_flat = attended.reshape(row_count, D)
    grad_flat = grad_whole.reshape(row_count, D)
    grad_attn = times_transpose(grad_flat, out_weight).astype(jnp.bfloat16).reshape(head_shape)
    grad_prob = jnp.einsum(
        "cfphd,cgphd->cphfg", grad_attn, value_heads, preferred_element_type=jnp.float32
    )
    grad_scores = (
        attn_prob * (grad_prob - jnp.sum(attn_prob * grad_prob, axis=-1, keepdims=True)) * factor
    ).astype(jnp.bfloat16)
    grad_query = jnp.einsum(
        "cphfg,cgphd->cfphd", grad_scores, key_heads, preferred_element_type=jnp.float32
    ).astype(jnp.bfloat16)
    grad_keys = jnp.einsum(
        "cphfg,cfphd->cgphd", grad_scores, query_heads, preferred_element_type=jnp.float32
    ).astype(jnp.bfloat16)
    grad_values = jnp.einsum(
        "cphfg,cfphd->cgphd", prob_bf, grad_attn, preferred_element_type=jnp.float32
    ).astype(jnp.bfloat16)
    grad_rows = jnp.concatenate(
        [
            grad_query.reshape(row_count, D),
            grad_keys.reshape(row_count, D),
            grad_values.reshape(row_count, D),
        ],
        axis=1,
    )
    grad_normed = times_transpose(grad_rows, qkv_weight)
    gain_term = jnp.sum(grad_normed * normal_hat, axis=0) * grad_scale
    bias_term = jnp.sum(grad_normed, axis=0) * grad_scale
    grad_hat = grad_normed * norm_gain
    grad_norm_in = (
        inv_std
        * (
            grad_hat
            - jnp.mean(grad_hat, axis=1, keepdims=True)
            - normal_hat * jnp.mean(grad_hat * normal_hat, axis=1, keepdims=True)
        )
    ).astype(jnp.bfloat16)
    returned = lax.all_to_all(
        grad_norm_in.reshape(clip_count, frame_count, patch_count, D),
        "seq",
        split_axis=1,
        concat_axis=2,
        tiled=True,
    )
    grad_input = (grad_live.astype(jnp.float32) + returned.astype(jnp.float32)).astype(jnp.bfloat16)
    gain_part, bias_part = (
        lax.psum_scatter(gain_term, "seq", scatter_dimension=0, tiled=True),
        lax.psum_scatter(bias_term, "seq", scatter_dimension=0, tiled=True),
    )
    upper_rows = contract_rows(normed, grad_rows)
    lower_rows = contract_rows(attn_flat, grad_flat)
    local_rows = lax.psum_scatter(
        (jnp.concatenate([upper_rows, lower_rows], axis=1) * grad_scale).astype(jnp.bfloat16),
        "seq",
        scatter_dimension=0,
        tiled=True,
    )
    summed, grad_gain, grad_bias = (
        lax.psum(local_rows, "rep").astype(jnp.float32),
        lax.psum(gain_part.astype(jnp.bfloat16), "rep").astype(jnp.float32),
        lax.psum(bias_part.astype(jnp.bfloat16), "rep").astype(jnp.float32),
    )
    return (grad_input, summed[:, : 3 * D], summed[:, 3 * D :], grad_gain, grad_bias)


def solution(mesh):
    return jax.shard_map(
        local,
        mesh=mesh,
        in_specs=(
            P("rep", "seq", None, None),
            P("rep", "seq", None, None),
            P("rep"),
            P("rep", None, None),
            P("rep", None),
            P(),
            P(),
            P(),
            P(),
        ),
        out_specs=(P("rep", "seq", None, None), P("seq", None), P("seq", None), P("seq"), P("seq")),
        check_vma=False,
    )
```

profile of v0, /device:TPU:1, one launch (start us, length us, event | category | flops | bytes accessed | tf_op | source)
XLA Modules:
  0.0 487.2 jit_solution(3071239003530918051)
XLA Ops:
  7.2 2.9 copy.94
  10.1 12.0 %all-to-all-start = ((bf16[2,8,32,1024]{3,1,0,2:T(8,128)(2,1)}), bf16[2,8,32,1024]{3,1,0,2:T(8,128)(2,1)S(1)}, u32[]{:S(2)}, u32[]{:S(2)}) async-start(bf16[2,8,32,1024]{3,1,0,2:T(8,128)(2,1)} %copy.94), calls=%async_computation | async-start | bytes 2097152 | tf_op jit(solution)/shard_map/all_to_all | solution.py:59
  26.6 20.4 %all-to-all-done = bf16[2,8,32,1024]{3,1,0,2:T(8,128)(2,1)S(1)} async-done(((bf16[2,8,32,1024]{3,1,0,2:T(8,128)(2,1)}), bf16[2,8,32,1024]{3,1,0,2:T(8,128)(2,1)S(1)}, u32[]{:S(2)}, u32[]{:S(2)}) %all-to-all-start) | async-done | bytes 1048608 | tf_op jit(solution)/shard_map/all_to_all | solution.py:59
  47.0 8.5 %all-to-all-start.1 = ((bf16[2,8,32,1024]{3,1,0,2:T(8,128)(2,1)}), bf16[2,8,32,1024]{3,1,0,2:T(8,128)(2,1)}, u32[]{:S(2)}, u32[]{:S(2)}) async-start(bf16[2,8,32,1024]{3,1,0,2:T(8,128)(2,1)} %copy.108), calls=%async_computation.1 | async-start | bytes 2097152 | tf_op jit(solution)/shard_map/all_to_all | solution.py:60
  57.7 3.2 copy.99
  63.7 6.8 %convolution_convert_fusion = bf16[512,3072]{1,0:T(8,128)(2,1)S(1)} fusion(bf16[512,1024]{1,0:T(8,128)(2,1)S(1)} %add_convert_fusion, bf16[1024,3072]{1,0:T(8,128)(2,1)} %param.16), kind=kOutput, calls=%fused_computation.11 | convolution fusion | flops 3222798336 | bytes 10485760 | tf_op jit(solution)/shard_map/dot_general | solution.py:76
  74.5 3.6 copy.114
  78.1 2.6 all-to-all-done.1
  87.3 3.0 reshape.228
  90.2 2.5 copy.113
  92.8 2.9 reshape.226
  98.2 5.9 %fusion.70 = f32[2,16,256,256]{2,3,1,0:T(8,128)} fusion(bf16[2,256,16,64]{1,3,2,0:T(8,128)(2,1)S(1)} %copy.112, bf16[2,256,16,64]{1,3,2,0:T(8,128)(2,1)} %copy.113), kind=kOutput, calls=%fused_computation.79 | convolution fusion | flops 268435456 | bytes 10485760 | tf_op jit(solution)/shard_map/cfphd,cgphd->cphfg/dot_general | solution.py:94
  104.1 17.9 %fusion.69 = (f32[2,16,256]{2,1,0:T(8,128)S(1)}, f32[2,16,256,256]{2,3,1,0:T(8,128)}) fusion(pred[2,256,256]{1,2,0:T(8,128)(4,1)S(1)} %copy.104, bf16[2,256,16,64]{1,3,2,0:T(8,128)(2,1)S(1)} %copy-done.6, bf16[2,256,16,64]{1,3,2,0:T(8,128)(2,1)S(1)} %copy-done.5), kind=kOutput, calls=%fused_computation.78 | convolution fusion | flops 549454080 | bytes 10649600 | tf_op jit(solution)/shard_map/sub | solution.py:85
  122.0 14.1 %fusion.40 = bf16[2,256,1,16,64]{1,4,3,0,2:T(8,128)(2,1)} fusion(bf16[2,256,16,64]{1,3,2,0:T(8,128)(2,1)S(1)} %copy-done.5, f32[2,16,256,256]{2,3,1,0:T(8,128)} %fusion.70, f32[2,16,256,256]{2,3,1,0:T(8,128)} %get-tuple-element.32, f32[2,16,256]{2,1,0:T(8,128)S(1)} %get-tuple-element.31), kind=kOutput, calls=%fused_computation.39 | convolution fusion | flops 283648256 | bytes 18907136 | tf_op jit(solution)/shard_map/cphfg,cgphd->cfphd/dot_general | solution.py:100
  136.0 13.2 %fusion.37 = bf16[2,256,1,16,64]{1,4,3,0,2:T(8,128)(2,1)} fusion(bf16[2,256,16,64]{1,3,2,0:T(8,128)(2,1)S(1)} %copy-done.6, f32[2,16,256,256]{2,3,1,0:T(8,128)} %fusion.70, f32[2,16,256,256]{2,3,1,0:T(8,128)} %get-tuple-element.32, f32[2,16,256]{2,1,0:T(8,128)S(1)} %get-tuple-element.31), kind=kOutput, calls=%fused_computation.38 | convolution fusion | flops 283648256 | bytes 18907136 | tf_op jit(solution)/shard_map/cphfg,cfphd->cgphd/dot_general | solution.py:103
  149.2 4.9 %fusion.46 = bf16[2,256,1,16,64]{1,4,3,0,2:T(8,128)(2,1)S(1)} fusion(bf16[2,256,16,64]{1,3,2,0:T(8,128)(2,1)S(1)} %copy.112, f32[2,16,256,256]{2,3,1,0:T(8,128)} %get-tuple-element.32, f32[2,16,256]{2,1,0:T(8,128)S(1)} %get-tuple-element.31), kind=kOutput, calls=%fused_computation.41 | convolution fusion | flops 273154048 | bytes 10518528 | tf_op jit(solution)/shard_map/cphfg,cfphd->cgphd/dot_general | solution.py:106
  164.4 3.5 fusion.71
  167.9 4.3 fusion.2
  173.8 7.2 %multiply_reduce_fusion.1 = (f32[1024]{0:T(1024)S(1)}, f32[512]{0:T(512)S(1)}, f32[512]{0:T(512)S(1)}, f32[1024]{0:T(1024)S(1)}, f32[512,1024]{1,0:T(8,128)S(1)}) fusion(f32[2,32,8,1,1024]{4,2,1,0,3:T(8,128)S(1)} %copy-done.2, f32[512]{0:T(512)S(1)} %div.35, f32[512]{0:T(512)S(1)} %rsqrt.12, f32[1024]{0:T(1024)S(1)} %copy-done.14, ...), kind=kOutput, calls=%fused_computation.23 | convolution fusion | flops 3225940992 | bytes 13651968 | tf_op jit(solution)/shard_map/dot_general | solution.py:37
  183.8 8.2 %all-to-all-start.2 = ((bf16[2,256,1,1024]{3,0,2,1:T(2,128)(2,1)}), bf16[2,256,1,1024]{3,0,2,1:T(2,128)(2,1)}, u32[]{:S(2)}, u32[]{:S(2)}) async-start(bf16[2,256,1,1024]{3,0,2,1:T(2,128)(2,1)} %copy.123), calls=%async_computation.2 | async-start | bytes 2097152 | tf_op jit(solution)/shard_map/all_to_all | solution.py:129
  193.3 85.7 %all-reduce.2 = (bf16[1024]{0:T(1024)(128)(2,1)S(1)}, bf16[1024]{0:T(1024)(128)(2,1)S(1)}) all-reduce(f32[1024]{0:T(1024)S(1)} %get-tuple-element.35, f32[1024]{0:T(1024)S(1)} %get-tuple-element.34), channel_id=3, replica_groups=mesh['rep'=8,'seq'=32] {'seq'}, use_global_device_ids=true, to_apply=%region_11.12.clone | all-reduce | flops 2048 | bytes 12288
  279.1 26.3 %all-reduce.3 = (bf16[32]{0:T(256)(128)(2,1)S(1)}, bf16[32]{0:T(256)(128)(2,1)S(1)}) all-reduce(bf16[32]{0:T(256)(128)(2,1)S(1)} %dynamic-slice.7, bf16[32]{0:T(256)(128)(2,1)S(1)} %dynamic-slice.6), channel_id=1, replica_groups=mesh['rep'=8,'seq'=32] {'rep'}, use_global_device_ids=true, to_apply=%region_12.13 | all-reduce | flops 64 | bytes 256 | tf_op jit(solution)/shard_map/psum | solution.py:151
  306.4 102.4 %reduce-scatter.2.cloned.1.call-done = bf16[32,4096]{1,0:T(8,128)(2,1)} async-done(((bf16[1024,4096]{1,0:T(8,128)(2,1)}), bf16[32,4096]{1,0:T(8,128)(2,1)}) %reduce-scatter.2.cloned.1.call-update) | async-done | bytes 262160 | tf_op jit(solution)/shard_map/reduce_scatter | solution.py:143
  412.5 64.4 %all-reduce.6.cloned.1.call-done = bf16[32,4096]{1,0:T(8,128)(2,1)} async-done(((bf16[32,4096]{1,0:T(8,128)(2,1)}), bf16[32,4096]{1,0:T(8,128)(2,1)}) %all-reduce.6.cloned.1.call-update) | async-done | bytes 262160 | tf_op jit(solution)/shard_map/psum | solution.py:150
  (100 shorter events, 44.8 us)
Async XLA Ops:
  7.2 75.8 %copy-start = (bf16[1024,1024]{1,0:T(8,128)(2,1)S(1)}, bf16[1024,1024]{1,0:T(8,128)(2,1)}, u32[]{:S(2)}) copy-start(bf16[1024,1024]{1,0:T(8,128)(2,1)} %param.17) | copy-start | bytes 6291460
  7.2 18.6 %copy-start.16 = (s32[2,4,3]{1,0,2:T(2,128)S(1)}, s32[2,4,3]{1,0,2:T(2,128)}, u32[]{:S(2)}) copy-start(s32[2,4,3]{1,0,2:T(2,128)} %param.12) | copy-start | bytes 292
  7.2 18.6 %copy-start.17 = (s32[2,4]{1,0:T(2,128)S(1)}, s32[2,4]{1,0:T(2,128)}, u32[]{:S(2)}) copy-start(s32[2,4]{1,0:T(2,128)} %param.13) | copy-start | bytes 100
  10.1 36.9 %all-to-all-start = ((bf16[2,8,32,1024]{3,1,0,2:T(8,128)(2,1)}), bf16[2,8,32,1024]{3,1,0,2:T(8,128)(2,1)S(1)}, u32[]{:S(2)}, u32[]{:S(2)}) async-start(bf16[2,8,32,1024]{3,1,0,2:T(8,128)(2,1)} %copy.94), calls=%async_computation | async-start | bytes 2097152 | tf_op jit(solution)/shard_map/all_to_all | solution.py:59
  47.0 33.6 %all-to-all-start.1 = ((bf16[2,8,32,1024]{3,1,0,2:T(8,128)(2,1)}), bf16[2,8,32,1024]{3,1,0,2:T(8,128)(2,1)}, u32[]{:S(2)}, u32[]{:S(2)}) async-start(bf16[2,8,32,1024]{3,1,0,2:T(8,128)(2,1)} %copy.108), calls=%async_computation.1 | async-start | bytes 2097152 | tf_op jit(solution)/shard_map/all_to_all | solution.py:60
  55.5 353.4 %reduce-scatter.2.cloned.1.call-start = ((), (), s32[]{:S(2)}) async-start(), calls=%async_computation.4 | async-start | bytes 8650752 | tf_op jit(solution)/shard_map/reduce_scatter | solution.py:143
  55.9 5.8 %copy-start.14 = (f32[1024]{0:T(1024)S(1)}, f32[1024]{0:T(1024)}, u32[]{:S(2)}) copy-start(f32[1024]{0:T(1024)} %param.14) | copy-start | bytes 12292
  55.9 5.8 %copy-start.15 = (f32[1024]{0:T(1024)S(1)}, f32[1024]{0:T(1024)}, u32[]{:S(2)}) copy-start(f32[1024]{0:T(1024)} %param.15) | copy-start | bytes 12292
  63.7 6.8 %copy-start.7 = (bf16[512,1024]{1,0:T(8,128)(2,1)}, bf16[512,1024]{1,0:T(8,128)(2,1)S(1)}, u32[]{:S(2)}) copy-start(bf16[512,1024]{1,0:T(8,128)(2,1)S(1)} %add_convert_fusion) | copy-start | bytes 3145732
  98.2 5.9 %copy-start.5 = (bf16[2,256,16,64]{1,3,2,0:T(8,128)(2,1)S(1)}, bf16[2,256,16,64]{1,3,2,0:T(8,128)(2,1)}, u32[]{:S(2)}) copy-start(bf16[2,256,16,64]{1,3,2,0:T(8,128)(2,1)} %copy.114) | copy-start | bytes 3145732
  98.2 5.9 %copy-start.6 = (bf16[2,256,16,64]{1,3,2,0:T(8,128)(2,1)S(1)}, bf16[2,256,16,64]{1,3,2,0:T(8,128)(2,1)}, u32[]{:S(2)}) copy-start(bf16[2,256,16,64]{1,3,2,0:T(8,128)(2,1)} %copy.106) | copy-start | bytes 3145732
  149.2 4.9 %copy-start.3 = (bf16[2,256,16,64]{1,3,2,0:T(8,128)(2,1)S(1)}, bf16[2,256,16,64]{1,3,2,0:T(8,128)(2,1)}, u32[]{:S(2)}) copy-start(bf16[2,256,16,64]{1,3,2,0:T(8,128)(2,1)} %copy.113) | copy-start | bytes 3145732
  149.2 6.1 %copy-start.19 = (f32[2,16,256,256]{2,3,1,0:T(8,128)S(1)}, f32[2,16,256,256]{2,3,1,0:T(8,128)}, u32[]{:S(2)}) copy-start(f32[2,16,256,256]{2,3,1,0:T(8,128)} %get-tuple-element.32) | copy-start | bytes 25165828
  155.3 1.2 copy-start.12
  156.5 1.4 copy-start.11
  159.3 2.7 copy-start.10
  163.2 1.2 copy-start.8
  164.4 3.5 copy-start.13
  172.2 1.6 copy-start.2
  181.1 10.9 %copy-start.18 = (u32[256]{0:T(256)S(1)}, u32[256]{0:T(256)}, u32[]{:S(2)}) copy-start(u32[256]{0:T(256)} %constant.50) | copy-start | bytes 3076
  181.1 227.8 %copy-start.4 = (bf16[2,8,32,1024]{3,2,1,0:T(8,128)(2,1)S(1)}, bf16[2,8,32,1024]{3,2,1,0:T(8,128)(2,1)}, u32[]{:S(2)}) copy-start(bf16[2,8,32,1024]{3,2,1,0:T(8,128)(2,1)} %param.10) | copy-start | bytes 3145732
  181.7 298.4 %copy-start.1 = (bf16[1024,1024]{1,0:T(8,128)(2,1)S(1)}, bf16[1024,1024]{1,0:T(8,128)(2,1)}, u32[]{:S(2)}) copy-start(bf16[1024,1024]{1,0:T(8,128)(2,1)} %param.17) | copy-start | bytes 6291460
  183.8 225.1 %all-to-all-start.2 = ((bf16[2,256,1,1024]{3,0,2,1:T(2,128)(2,1)}), bf16[2,256,1,1024]{3,0,2,1:T(2,128)(2,1)}, u32[]{:S(2)}, u32[]{:S(2)}) async-start(bf16[2,256,1,1024]{3,0,2,1:T(2,128)(2,1)} %copy.123), calls=%async_computation.2 | async-start | bytes 2097152 | tf_op jit(solution)/shard_map/all_to_all | solution.py:129
  192.0 284.9 %all-reduce.6.cloned.1.call-start = ((), (), s32[]{:S(2)}) async-start(), calls=%async_computation.5 | async-start | bytes 524288 | tf_op jit(solution)/shard_map/psum | solution.py:150
  (1 other events, 1.0 us)
Sparse Core Ops, SparseCore 0:
  172.4 236.4 reduce-scatter.1
  411.2 65.6 all-reduce.5
where the time goes:
time: 493 us; the launch traced here: 487 us
  waiting for transfers between devices  190 us (39%)
  blocking collectives  112 us (23%)
  matrix products  77.4 us (16%)
  local copies, waits for them, and re-layouts  49 us (10%)
  starting transfers between devices  28.7 us (6%)
  between operations  16 us (3%)
  other arithmetic  14.2 us (3%)
    reduce_scatter x1, waiting for transfers between devices, local(): lax.psum_scatter((jnp.concatenate([upper_rows, lower_rows], axis=1) * gra...  102 us
    unnamed x1, blocking collectives  85.7 us
    psum x1, waiting for transfers between devices, local(): lax.psum(local_rows, 'rep').astype(jnp.float32)  64.4 us
    psum x1, blocking collectives, local(): lax.psum(gain_part.astype(jnp.bfloat16), 'rep').astype(jnp.float32)  26.3 us
    all_to_all x1, waiting for transfers between devices, local(): lax.all_to_all(tokens, 'seq', split_axis=2, concat_axis=1, tiled=True)  20.4 us
    another operation x8, local copies, waits for them, and re-layouts  19.9 us
    sub x1, matrix products, local(): exp_scores = jnp.where(allowed, jnp.exp(scores - row_max), 0.0)  17.9 us
    dot_general x1, matrix products, local(): jnp.einsum('cphfg,cgphd->cfphd', grad_scores, key_heads, preferred_elemen...  14.1 us
  transfers between devices with their start and end apart: 5, of which 4 were waited for; matrix products, arithmetic and copies ran while one was open for 9% of the time, Pallas kernels for 0%

commit v1 on v0

--- a/solution.py
+++ b/solution.py
@@ -4,7 +4,8 @@
 import jax
 import jax.numpy as jnp
 from jax import lax
-from jax.sharding import PartitionSpec as P
+from jax.sharding import Mesh, PartitionSpec as P
+import numpy as np
 
 D = 1024
 HEADS = 16
@@ -50,14 +51,14 @@
     qkv_weight,
     out_weight,
 ):
-    seq_size = lax.axis_size("seq")
-    rep_size = lax.axis_size("rep")
+    seq_size = lax.axis_size(("y", "z"))
+    rep_size = lax.axis_size(("x", "core"))
     clip_count = tokens.shape[0]
     live_slot = jnp.arange(clip_count) < clip_counts[0]
     grad_live = jnp.where(live_slot[:, None, None, None], cotangent, jnp.zeros_like(cotangent))
     gathered, grad_whole = (
-        lax.all_to_all(tokens, "seq", split_axis=2, concat_axis=1, tiled=True),
-        lax.all_to_all(grad_live, "seq", split_axis=2, concat_axis=1, tiled=True),
+        lax.all_to_all(tokens, ("y", "z"), split_axis=2, concat_axis=1, tiled=True),
+        lax.all_to_all(grad_live, ("y", "z"), split_axis=2, concat_axis=1, tiled=True),
     )
     frame_count = gathered.shape[1]
     patch_count = gathered.shape[2]
@@ -128,47 +129,60 @@
     ).astype(jnp.bfloat16)
     returned = lax.all_to_all(
         grad_norm_in.reshape(clip_count, frame_count, patch_count, D),
-        "seq",
+        ("y", "z"),
         split_axis=1,
         concat_axis=2,
         tiled=True,
     )
     grad_input = (grad_live.astype(jnp.float32) + returned.astype(jnp.float32)).astype(jnp.bfloat16)
-    gain_part, bias_part = (
-        lax.psum_scatter(gain_term, "seq", scatter_dimension=0, tiled=True),
-        lax.psum_scatter(bias_term, "seq", scatter_dimension=0, tiled=True),
-    )
+    seq_index = lax.axis_index(("y", "z"))
+    side_terms = lax.psum(jnp.stack([gain_term, bias_term]), ("x", "core", "y", "z"))
+    side_terms = lax.dynamic_slice_in_dim(side_terms, seq_index * (D // seq_size), D // seq_size, axis=1)
     upper_rows = contract_rows(normed, grad_rows)
     lower_rows = contract_rows(attn_flat, grad_flat)
-    local_rows = lax.psum_scatter(
-        (jnp.concatenate([upper_rows, lower_rows], axis=1) * grad_scale).astype(jnp.bfloat16),
-        "seq",
-        scatter_dimension=0,
-        tiled=True,
+    stacked = (jnp.concatenate([upper_rows, lower_rows], axis=1) * grad_scale).astype(jnp.bfloat16)
+    x_size = lax.axis_size("x")
+    width = stacked.shape[1] // (2 * x_size)
+    split = stacked.reshape(D, x_size, 2, width)
+    core = lax.axis_index("core")
+    mine = lax.dynamic_index_in_dim(split, core, axis=2, keepdims=False)
+    other = lax.dynamic_index_in_dim(split, 1 - core, axis=2, keepdims=False)
+    got = lax.ppermute(other, "core", [(0, 1), (1, 0)])
+    merged = (mine.astype(jnp.float32) + got.astype(jnp.float32)).astype(jnp.bfloat16)
+    merged = lax.psum_scatter(merged, "y", scatter_dimension=0, tiled=True)
+    merged = lax.psum_scatter(merged, "z", scatter_dimension=0, tiled=True)
+    merged = lax.psum_scatter(merged, "x", scatter_dimension=1, tiled=True)
+    summed = lax.all_gather(
+        merged.reshape(merged.shape[0], width), ("x", "core"), axis=1, tiled=True
+    ).astype(jnp.float32)
+    return (grad_input, summed[:, : 3 * D], summed[:, 3 * D :], side_terms[0], side_terms[1])
+
+
+def fine_mesh(mesh):
+    devices = np.asarray(mesh.devices)
+    rep_size, seq_size = devices.shape
+    y_size = len({device.coords[1] for device in devices.flat})
+    return Mesh(
+        devices.reshape(rep_size // 2, 2, y_size, seq_size // y_size), ("x", "core", "y", "z")
     )
-    summed, grad_gain, grad_bias = (
-        lax.psum(local_rows, "rep").astype(jnp.float32),
-        lax.psum(gain_part.astype(jnp.bfloat16), "rep").astype(jnp.float32),
-        lax.psum(bias_part.astype(jnp.bfloat16), "rep").astype(jnp.float32),
-    )
-    return (grad_input, summed[:, : 3 * D], summed[:, 3 * D :], grad_gain, grad_bias)
 
 
 def solution(mesh):
+    rep, seq = ("x", "core"), ("y", "z")
     return jax.shard_map(
         local,
-        mesh=mesh,
+        mesh=fine_mesh(mesh),
         in_specs=(
-            P("rep", "seq", None, None),
-            P("rep", "seq", None, None),
-            P("rep"),
-            P("rep", None, None),
-            P("rep", None),
+            P(rep, seq, None, None),
+            P(rep, seq, None, None),
+            P(rep),
+            P(rep, None, None),
+            P(rep, None),
             P(),
             P(),
             P(),
             P(),
         ),
-        out_specs=(P("rep", "seq", None, None), P("seq", None), P("seq", None), P("seq"), P("seq")),
+        out_specs=(P(rep, seq, None, None), P(seq, None), P(seq, None), P(seq), P(seq)),
         check_vma=False,
     )

time: 493 us -> 406 us (0.82)
  waiting for transfers between devices: 190 us -> 79.5 us
  local copies, waits for them, and re-layouts: 49 us -> 89 us
  blocking collectives: 112 us -> 94.8 us
  matrix products: 77.4 us -> 67.4 us
  other arithmetic: 14.2 us -> 21.6 us
    unnamed x1 -> x0, blocking collectives: 85.7 us -> none
    psum x1 -> x0, waiting for transfers between devices: 64.4 us -> none  [local(): lax.psum(local_rows, 'rep').astype(jnp.float32)]
    reduce_scatter x1 -> x3, waiting for transfers between devices: 102 us -> 49.7 us  [the longest x1 35 us: local(): merged = lax.psum_scatter(merged, 'y', scatter_dimension=0, tiled=True)]
    psum x1, blocking collectives: 26.3 us -> 79 us  [local(): lax.psum(jnp.stack([gain_term, bias_term]), ('x', 'core', 'y', 'z'))]
    dynamic_slice x0 -> x3, local copies, waits for them, and re-layouts: none -> 25.8 us  [the longest x1 19.9 us: local(): mine = lax.dynamic_index_in_dim(split, core, axis=2, keepdims=False)]
    all_gather x0 -> x1, blocking collectives: none -> 15.8 us  [local(): lax.all_gather(merged.reshape(merged.shape[0], width), ('x', 'core'), axi...]
    convert_element_type x0 -> x1, local copies, waits for them, and re-layouts: none -> 14.4 us  [local(): (jnp.concatenate([upper_rows, lower_rows], axis=1) * grad_scale).astype(j...]
    sub x1, matrix products: 17.9 us -> 6.1 us  [local(): exp_scores = jnp.where(allowed, jnp.exp(scores - row_max), 0.0)]
  transfers between devices with their start and end apart: 5 -> 7, of which waited for: 4 -> 5; matrix products, arithmetic and copies ran while one was open for 9% -> 11% of each run, Pallas kernels for 0% -> 0%
where the time goes in v1:
time: 406 us; the launch traced here: 401 us
  blocking collectives  94.8 us (23%)
  local copies, waits for them, and re-layouts  89 us (22%)
  waiting for transfers between devices  79.5 us (20%)
  matrix products  67.4 us (17%)
  starting transfers between devices  33.6 us (8%)
  other arithmetic  21.6 us (5%)
  between operations  15.1 us (4%)
    psum x1, blocking collectives, local(): lax.psum(jnp.stack([gain_term, bias_term]), ('x', 'core', 'y', 'z'))  79 us
    reduce_scatter x1, waiting for transfers between devices, local(): merged = lax.psum_scatter(merged, 'y', scatter_dimension=0, tiled=True)  35 us
    all_to_all x1, waiting for transfers between devices, local(): lax.all_to_all(tokens, ('y', 'z'), split_axis=2, concat_axis=1, tiled=True)  20.4 us
    dynamic_slice x1, local copies, waits for them, and re-layouts, local(): mine = lax.dynamic_index_in_dim(split, core, axis=2, keepdims=False)  19.9 us
    another operation x8, local copies, waits for them, and re-layouts  19.9 us
    all_gather x1, blocking collectives, local(): lax.all_gather(merged.reshape(merged.shape[0], width), ('x', 'core'), axi...  15.8 us
    reduce_scatter x1, waiting for transfers between devices, local(): merged = lax.psum_scatter(merged, 'x', scatter_dimension=1, tiled=True)  14.7 us
    convert_element_type x1, local copies, waits for them, and re-layouts, local(): (jnp.concatenate([upper_rows, lower_rows], axis=1) * grad_scale).astype(j...  14.4 us
  transfers between devices with their start and end apart: 7, of which 5 were waited for; matrix products, arithmetic and copies ran while one was open for 11% of the time, Pallas kernels for 0%

profile of v1, /device:TPU:1, one launch (start us, length us, event | category | flops | bytes accessed | tf_op | source)
XLA Modules:
  0.0 401.0 jit_solution(5838071315834525960)
XLA Ops:
  10.1 12.0 %all-to-all-start = ((bf16[2,8,32,1024]{3,1,0,2:T(8,128)(2,1)}), bf16[2,8,32,1024]{3,1,0,2:T(8,128)(2,1)S(1)}, u32[]{:S(2)}, u32[]{:S(2)}) async-start(bf16[2,8,32,1024]{3,1,0,2:T(8,128)(2,1)} %copy.100), calls=%async_computation | async-start | bytes 2097152 | tf_op jit(solution)/shard_map/all_to_all | solution.py:60
  26.6 20.4 %all-to-all-done = bf16[2,8,32,1024]{3,1,0,2:T(8,128)(2,1)S(1)} async-done(((bf16[2,8,32,1024]{3,1,0,2:T(8,128)(2,1)}), bf16[2,8,32,1024]{3,1,0,2:T(8,128)(2,1)S(1)}, u32[]{:S(2)}, u32[]{:S(2)}) %all-to-all-start) | async-done | bytes 1048608 | tf_op jit(solution)/shard_map/all_to_all | solution.py:60
  47.0 8.5 %all-to-all-start.1 = ((bf16[2,8,32,1024]{3,1,0,2:T(8,128)(2,1)}), bf16[2,8,32,1024]{3,1,0,2:T(8,128)(2,1)}, u32[]{:S(2)}, u32[]{:S(2)}) async-start(bf16[2,8,32,1024]{3,1,0,2:T(8,128)(2,1)} %copy.114), calls=%async_computation.1 | async-start | bytes 2097152 | tf_op jit(solution)/shard_map/all_to_all | solution.py:61
  63.7 6.8 %convolution_convert_fusion = bf16[512,3072]{1,0:T(8,128)(2,1)S(1)} fusion(bf16[512,1024]{1,0:T(8,128)(2,1)S(1)} %add_convert_fusion, bf16[1024,3072]{1,0:T(8,128)(2,1)} %param.16), kind=kOutput, calls=%fused_computation.13 | convolution fusion | flops 3222798336 | bytes 10485760 | tf_op jit(solution)/shard_map/dot_general | solution.py:77
  74.5 3.6 copy.120
  98.3 5.9 %fusion.71 = f32[2,16,256,256]{2,3,1,0:T(8,128)} fusion(bf16[2,256,16,64]{1,3,2,0:T(8,128)(2,1)S(1)} %copy.118, bf16[2,256,16,64]{1,3,2,0:T(8,128)(2,1)} %copy.119), kind=kOutput, calls=%fused_computation.88 | convolution fusion | flops 268435456 | bytes 10485760 | tf_op jit(solution)/shard_map/cfphd,cgphd->cphfg/dot_general | solution.py:95
  104.2 6.1 %fusion.70 = (f32[2,16,256]{2,1,0:T(8,128)S(1)}, f32[2,16,256,256]{2,3,1,0:T(8,128)}) fusion(pred[2,256,256]{1,2,0:T(8,128)(4,1)S(1)} %copy.110, bf16[2,256,16,64]{1,3,2,0:T(8,128)(2,1)S(1)} %copy-done.7, bf16[2,256,16,64]{1,3,2,0:T(8,128)(2,1)S(1)} %copy-done.6), kind=kOutput, calls=%fused_computation.87 | convolution fusion | flops 549454080 | bytes 10649600 | tf_op jit(solution)/shard_map/sub | solution.py:86
  110.3 14.1 %fusion.41 = bf16[2,256,1,16,64]{1,4,3,0,2:T(8,128)(2,1)} fusion(bf16[2,256,16,64]{1,3,2,0:T(8,128)(2,1)S(1)} %copy-done.6, f32[2,16,256,256]{2,3,1,0:T(8,128)} %fusion.71, f32[2,16,256,256]{2,3,1,0:T(8,128)} %get-tuple-element.32, f32[2,16,256]{2,1,0:T(8,128)S(1)} %get-tuple-element.31), kind=kOutput, calls=%fused_computation.43 | convolution fusion | flops 283648256 | bytes 18907136 | tf_op jit(solution)/shard_map/cphfg,cgphd->cfphd/dot_general | solution.py:101
  124.3 13.2 %fusion.38 = bf16[2,256,1,16,64]{1,4,3,0,2:T(8,128)(2,1)} fusion(bf16[2,256,16,64]{1,3,2,0:T(8,128)(2,1)S(1)} %copy-done.7, f32[2,16,256,256]{2,3,1,0:T(8,128)} %fusion.71, f32[2,16,256,256]{2,3,1,0:T(8,128)} %get-tuple-element.32, f32[2,16,256]{2,1,0:T(8,128)S(1)} %get-tuple-element.31), kind=kOutput, calls=%fused_computation.42 | convolution fusion | flops 283648256 | bytes 18907136 | tf_op jit(solution)/shard_map/cphfg,cfphd->cgphd/dot_general | solution.py:104
  137.5 4.9 %fusion.47 = bf16[2,256,1,16,64]{1,4,3,0,2:T(8,128)(2,1)S(1)} fusion(bf16[2,256,16,64]{1,3,2,0:T(8,128)(2,1)S(1)} %copy.118, f32[2,16,256,256]{2,3,1,0:T(8,128)} %get-tuple-element.32, f32[2,16,256]{2,1,0:T(8,128)S(1)} %get-tuple-element.31), kind=kOutput, calls=%fused_computation.45 | convolution fusion | flops 273154048 | bytes 10518528 | tf_op jit(solution)/shard_map/cphfg,cfphd->cgphd/dot_general | solution.py:107
  152.7 3.5 fusion.72
  156.2 4.3 %fusion.2 = bf16[1024,4096]{1,0:T(8,128)(2,1)} fusion(f32[1024,1024]{1,0:T(8,128)S(1)} %fusion.73, f32[1024,3072]{1,0:T(8,128)S(1)} %fusion.72), kind=kLoop, calls=%fused_computation.3 | loop fusion | flops 12582912 | bytes 25165824 | tf_op jit(solution)/shard_map/convert_element_type | solution.py:143
  160.5 14.4 %convert_element_type.146 = bf16[1024,4,2,512]{3,2,1,0:T(2,128)(2,1)} reshape(bf16[1024,4096]{1,0:T(8,128)(2,1)} %fusion.2) | data formatting | bytes 16777216 | tf_op jit(solution)/shard_map/convert_element_type | solution.py:143
  175.0 19.9 %constant_dynamic-slice_fusion.2 = (bf16[1024,4,1,512]{3,2,1,0:T(2,128)(2,1)S(1)}, bf16[1024,4,1,512]{3,2,1,0:T(2,128)(2,1)}) fusion(bf16[1024,4,2,512]{3,2,1,0:T(2,128)(2,1)} %convert_element_type.146, s32[]{:T(128)S(6)} %select_n.39, s32[]{:T(128)S(6)} %select_n.40), kind=kLoop, calls=%fused_computation.76 | loop fusion | bytes 16777224 | tf_op jit(solution)/shard_map/jit(dynamic_index_in_dim)/dynamic_slice | solution.py:148
  194.9 5.8 %copy.167 = bf16[1024,4,1,512]{3,0,1,2:T(8,128)(2,1)S(1)} copy(bf16[1024,4,1,512]{3,2,1,0:T(2,128)(2,1)} %get-tuple-element.25) | data formatting | bytes 8388608 | tf_op jit(solution)/shard_map/jit(dynamic_index_in_dim)/dynamic_slice | solution.py:149
  200.7 4.6 %collective-permute-start = (bf16[1024,4,512]{2,0,1:T(8,128)(2,1)S(1)}, bf16[1024,4,512]{2,0,1:T(8,128)(2,1)S(1)}, u32[]{:S(2)}, u32[]{:S(2)}) collective-permute-start(bf16[1024,4,512]{2,0,1:T(8,128)(2,1)S(1)} %bitcast.120), channel_id=1, source_target_pairs={{0,32},{32,0},{1,33},{33,1},{2,34},{34,2},{3,35},{35,3},{4,36},{36... | collective-permute-start | bytes 12582920 | tf_op jit(solution)/shard_map/ppermute | solution.py:150
  205.3 6.8 %collective-permute-done = bf16[1024,4,512]{2,0,1:T(8,128)(2,1)S(1)} collective-permute-done((bf16[1024,4,512]{2,0,1:T(8,128)(2,1)S(1)}, bf16[1024,4,512]{2,0,1:T(8,128)(2,1)S(1)}, u32[]{:S(2)}, u32[]{:S(2)}) %collective-permute-start) | collective-permute-done | bytes 4194336 | tf_op jit(solution)/shard_map/ppermute | solution.py:150
  214.1 6.7 %fusion.3 = bf16[1024,4,512]{2,0,1:T(8,128)(2,1)} fusion(bf16[1024,4,512]{2,0,1:T(8,128)(2,1)} %copy-done.5, bf16[1024,4,1,512]{3,2,1,0:T(2,128)(2,1)S(1)} %get-tuple-element.24), kind=kLoop, calls=%fused_computation.5 | loop fusion | flops 8388608 | bytes 12582912 | tf_op jit(solution)/shard_map/convert_element_type | solution.py:151
  222.4 9.0 %multiply_reduce_fusion.1 = (f32[1024]{0:T(1024)S(1)}, f32[512]{0:T(512)S(1)}, f32[512]{0:T(512)S(1)}, f32[1024]{0:T(1024)S(1)}, f32[512,1024]{1,0:T(8,128)}) fusion(f32[2,32,8,1,1024]{4,2,1,0,3:T(8,128)S(1)} %copy-done.2, f32[512]{0:T(512)S(1)} %div.35, f32[512]{0:T(512)S(1)} %rsqrt.12, f32[1024]{0:T(1024)S(1)} %copy-done.15, ...), kind=kOutput, calls=%fused_computation.27 | convolution fusion | flops 3225940992 | bytes 13651968 | tf_op jit(solution)/shard_map/dot_general | solution.py:38
  231.4 35.0 %reduce-scatter.4.cloned.1.call-done = bf16[256,4,512]{2,0,1:T(8,128)(2,1)} async-done(((bf16[1024,4,512]{2,0,1:T(8,128)(2,1)}), bf16[256,4,512]{2,0,1:T(8,128)(2,1)}) %reduce-scatter.4.cloned.1.call-update) | async-done | bytes 1048592 | tf_op jit(solution)/shard_map/reduce_scatter | solution.py:152
  270.8 8.2 %all-to-all-start.2 = ((bf16[2,256,1,1024]{3,0,2,1:T(2,128)(2,1)}), bf16[2,256,1,1024]{3,0,2,1:T(2,128)(2,1)}, u32[]{:S(2)}, u32[]{:S(2)}) async-start(bf16[2,256,1,1024]{3,0,2,1:T(2,128)(2,1)} %copy.129), calls=%async_computation.2 | async-start | bytes 2097152 | tf_op jit(solution)/shard_map/all_to_all | solution.py:130
  279.1 79.0 %psum.7 = f32[2,1024]{1,0:T(2,128)S(1)} all-reduce(f32[2,1024]{1,0:T(2,128)S(1)} %pad_maximum_fusion), channel_id=1, replica_groups=mesh['x'=4,'core'=2,'y'=4,'z'=8] {'x','core','y','z'}, use_global_device_ids=true, to_apply=%region_13.14 | all-reduce | flops 2048 | bytes 16384 | tf_op jit(solution)/shard_map/psum | solution.py:139
  362.3 14.7 %reduce-scatter.8.cloned.1.call-done = bf16[32,1,512]{2,0,1:T(8,128)(2,1)} async-done(((bf16[32,4,512]{2,0,1:T(8,128)(2,1)}), bf16[32,1,512]{2,0,1:T(8,128)(2,1)}) %reduce-scatter.8.cloned.1.call-update) | async-done | bytes 32784 | tf_op jit(solution)/shard_map/reduce_scatter | solution.py:154
  377.0 15.8 %all-gather = bf16[32,1,4096]{2,0,1:T(8,128)(2,1)S(1)} all-gather(bf16[32,1,512]{2,0,1:T(8,128)(2,1)} %reduce-scatter.8.cloned.1.call-done), channel_id=2, replica_groups=mesh['x'=4,'core'=2,'y'=4,'z'=8] {'x','core'}, dimensions={2}, use_global_device_ids=true | all-gather | bytes 294912 | tf_op jit(solution)/shard_map/all_gather | solution.py:155
  (108 shorter events, 62.8 us)
Async XLA Ops:
  7.2 75.8 %copy-start = (bf16[1024,1024]{1,0:T(8,128)(2,1)S(1)}, bf16[1024,1024]{1,0:T(8,128)(2,1)}, u32[]{:S(2)}) copy-start(bf16[1024,1024]{1,0:T(8,128)(2,1)} %param.17) | copy-start | bytes 6291460
  7.2 18.6 %copy-start.17 = (s32[2,4,3]{1,0,2:T(2,128)S(1)}, s32[2,4,3]{1,0,2:T(2,128)}, u32[]{:S(2)}) copy-start(s32[2,4,3]{1,0,2:T(2,128)} %param.12) | copy-start | bytes 292
  7.2 18.6 %copy-start.18 = (s32[2,4]{1,0:T(2,128)S(1)}, s32[2,4]{1,0:T(2,128)}, u32[]{:S(2)}) copy-start(s32[2,4]{1,0:T(2,128)} %param.13) | copy-start | bytes 100
  10.1 36.9 %all-to-all-start = ((bf16[2,8,32,1024]{3,1,0,2:T(8,128)(2,1)}), bf16[2,8,32,1024]{3,1,0,2:T(8,128)(2,1)S(1)}, u32[]{:S(2)}, u32[]{:S(2)}) async-start(bf16[2,8,32,1024]{3,1,0,2:T(8,128)(2,1)} %copy.100), calls=%async_computation | async-start | bytes 2097152 | tf_op jit(solution)/shard_map/all_to_all | solution.py:60
  47.0 33.6 %all-to-all-start.1 = ((bf16[2,8,32,1024]{3,1,0,2:T(8,128)(2,1)}), bf16[2,8,32,1024]{3,1,0,2:T(8,128)(2,1)}, u32[]{:S(2)}, u32[]{:S(2)}) async-start(bf16[2,8,32,1024]{3,1,0,2:T(8,128)(2,1)} %copy.114), calls=%async_computation.1 | async-start | bytes 2097152 | tf_op jit(solution)/shard_map/all_to_all | solution.py:61
  55.5 211.0 %reduce-scatter.4.cloned.1.call-start = ((), (), s32[]{:S(2)}) async-start(), calls=%async_computation.6 | async-start | bytes 5242880 | tf_op jit(solution)/shard_map/reduce_scatter | solution.py:152
  55.9 5.8 %copy-start.15 = (f32[1024]{0:T(1024)S(1)}, f32[1024]{0:T(1024)}, u32[]{:S(2)}) copy-start(f32[1024]{0:T(1024)} %param.14) | copy-start | bytes 12292
  55.9 5.8 %copy-start.16 = (f32[1024]{0:T(1024)S(1)}, f32[1024]{0:T(1024)}, u32[]{:S(2)}) copy-start(f32[1024]{0:T(1024)} %param.15) | copy-start | bytes 12292
  63.7 6.8 %copy-start.8 = (bf16[512,1024]{1,0:T(8,128)(2,1)}, bf16[512,1024]{1,0:T(8,128)(2,1)S(1)}, u32[]{:S(2)}) copy-start(bf16[512,1024]{1,0:T(8,128)(2,1)S(1)} %add_convert_fusion) | copy-start | bytes 3145732
  98.3 5.9 %copy-start.6 = (bf16[2,256,16,64]{1,3,2,0:T(8,128)(2,1)S(1)}, bf16[2,256,16,64]{1,3,2,0:T(8,128)(2,1)}, u32[]{:S(2)}) copy-start(bf16[2,256,16,64]{1,3,2,0:T(8,128)(2,1)} %copy.120) | copy-start | bytes 3145732
  98.3 5.9 %copy-start.7 = (bf16[2,256,16,64]{1,3,2,0:T(8,128)(2,1)S(1)}, bf16[2,256,16,64]{1,3,2,0:T(8,128)(2,1)}, u32[]{:S(2)}) copy-start(bf16[2,256,16,64]{1,3,2,0:T(8,128)(2,1)} %copy.112) | copy-start | bytes 3145732
  137.5 4.9 %copy-start.3 = (bf16[2,256,16,64]{1,3,2,0:T(8,128)(2,1)S(1)}, bf16[2,256,16,64]{1,3,2,0:T(8,128)(2,1)}, u32[]{:S(2)}) copy-start(bf16[2,256,16,64]{1,3,2,0:T(8,128)(2,1)} %copy.119) | copy-start | bytes 3145732
  137.5 6.1 %copy-start.19 = (f32[2,16,256,256]{2,3,1,0:T(8,128)S(1)}, f32[2,16,256,256]{2,3,1,0:T(8,128)}, u32[]{:S(2)}) copy-start(f32[2,16,256,256]{2,3,1,0:T(8,128)} %get-tuple-element.32) | copy-start | bytes 25165828
  144.8 1.4 copy-start.12
  147.6 2.7 copy-start.11
  152.7 3.5 copy-start.14
  200.7 11.4 %collective-permute-start = (bf16[1024,4,512]{2,0,1:T(8,128)(2,1)S(1)}, bf16[1024,4,512]{2,0,1:T(8,128)(2,1)S(1)}, u32[]{:S(2)}, u32[]{:S(2)}) collective-permute-start(bf16[1024,4,512]{2,0,1:T(8,128)(2,1)S(1)} %bitcast.120), channel_id=1, source_target_pairs={{0,32},{32,0},{1,33},{33,1},{2,34},{34,2},{3,35},{35,3},{4,36},{36... | collective-permute-start | bytes 12582920 | tf_op jit(solution)/shard_map/ppermute | solution.py:150
  212.1 2.0 copy-start.5
  220.8 1.6 copy-start.2
  220.8 137.8 %reduce-scatter.6.cloned.1.call-start = ((), (), s32[]{:S(2)}) async-start(), calls=%async_computation.7 | async-start | bytes 1179648 | tf_op jit(solution)/shard_map/reduce_scatter | solution.py:153
  266.5 92.2 %copy-start.4 = (bf16[2,8,32,1024]{3,2,1,0:T(8,128)(2,1)S(1)}, bf16[2,8,32,1024]{3,2,1,0:T(8,128)(2,1)}, u32[]{:S(2)}) copy-start(bf16[2,8,32,1024]{3,2,1,0:T(8,128)(2,1)} %param.10) | copy-start | bytes 3145732
  270.8 87.8 %all-to-all-start.2 = ((bf16[2,256,1,1024]{3,0,2,1:T(2,128)(2,1)}), bf16[2,256,1,1024]{3,0,2,1:T(2,128)(2,1)}, u32[]{:S(2)}, u32[]{:S(2)}) async-start(bf16[2,256,1,1024]{3,0,2,1:T(2,128)(2,1)} %copy.129), calls=%async_computation.2 | async-start | bytes 2097152 | tf_op jit(solution)/shard_map/all_to_all | solution.py:130
  279.0 115.3 %copy-start.1 = (bf16[1024,1024]{1,0:T(8,128)(2,1)S(1)}, bf16[1024,1024]{1,0:T(8,128)(2,1)}, u32[]{:S(2)}) copy-start(bf16[1024,1024]{1,0:T(8,128)(2,1)} %param.17) | copy-start | bytes 6291460
  279.0 97.9 %reduce-scatter.8.cloned.1.call-start = ((), (), s32[]{:S(2)}) async-start(), calls=%async_computation.8 | async-start | bytes 163840 | tf_op jit(solution)/shard_map/reduce_scatter | solution.py:154
  (3 other events, 3.5 us)
Sparse Core Ops, SparseCore 0:
  221.0 45.4 reduce-scatter.3
  269.0 47.0 reduce-scatter.5
  358.8 18.1 reduce-scatter.7

commit v2 on v1

--- a/solution.py
+++ b/solution.py
@@ -135,21 +135,29 @@
         tiled=True,
     )
     grad_input = (grad_live.astype(jnp.float32) + returned.astype(jnp.float32)).astype(jnp.bfloat16)
-    seq_index = lax.axis_index(("y", "z"))
-    side_terms = lax.psum(jnp.stack([gain_term, bias_term]), ("x", "core", "y", "z"))
-    side_terms = lax.dynamic_slice_in_dim(side_terms, seq_index * (D // seq_size), D // seq_size, axis=1)
-    upper_rows = contract_rows(normed, grad_rows)
-    lower_rows = contract_rows(attn_flat, grad_flat)
-    stacked = (jnp.concatenate([upper_rows, lower_rows], axis=1) * grad_scale).astype(jnp.bfloat16)
+    side_terms = jnp.stack([gain_term, bias_term]).reshape(2, seq_size, D // seq_size)
+    side_terms = lax.all_to_all(side_terms, ("y", "z"), split_axis=1, concat_axis=1, tiled=True)
+    side_terms = lax.psum(jnp.sum(side_terms, axis=1), ("x", "core"))
     x_size = lax.axis_size("x")
-    width = stacked.shape[1] // (2 * x_size)
-    split = stacked.reshape(D, x_size, 2, width)
+    width = (3 * D + D) // (2 * x_size)
     core = lax.axis_index("core")
-    mine = lax.dynamic_index_in_dim(split, core, axis=2, keepdims=False)
-    other = lax.dynamic_index_in_dim(split, 1 - core, axis=2, keepdims=False)
-    got = lax.ppermute(other, "core", [(0, 1), (1, 0)])
+
+    def half_of(index):
+        grad_part = lax.dynamic_index_in_dim(
+            grad_rows.reshape(row_count, 3 * D // (2 * width), 2, width), index, axis=2, keepdims=False
+        ).reshape(row_count, 3 * D // 2)
+        flat_part = lax.dynamic_slice_in_dim(grad_flat, index * width, width, axis=1)
+        return (
+            jnp.concatenate(
+                [contract_rows(normed, grad_part), contract_rows(attn_flat, flat_part)], axis=1
+            )
+            * grad_scale
+        ).astype(jnp.bfloat16)
+
+    mine = half_of(core)
+    got = lax.ppermute(half_of(1 - core), "core", [(0, 1), (1, 0)])
     merged = (mine.astype(jnp.float32) + got.astype(jnp.float32)).astype(jnp.bfloat16)
-    merged = lax.psum_scatter(merged, "y", scatter_dimension=0, tiled=True)
+    merged = lax.psum_scatter(merged.reshape(D, x_size, width), "y", scatter_dimension=0, tiled=True)
     merged = lax.psum_scatter(merged, "z", scatter_dimension=0, tiled=True)
     merged = lax.psum_scatter(merged, "x", scatter_dimension=1, tiled=True)
     summed = lax.all_gather(

time: 406 us -> 337 us (0.83)
  blocking collectives: 94.8 us -> 29.1 us
  local copies, waits for them, and re-layouts: 89 us -> 65.5 us
  waiting for transfers between devices: 79.5 us -> 98.9 us
  other arithmetic: 21.6 us -> 14.3 us
  starting transfers between devices: 33.6 us -> 39.7 us
    psum x1, blocking collectives: 79 us -> 13.3 us  [local(): side_terms = lax.psum(jnp.sum(side_terms, axis=1), ('x', 'core'))]
    dynamic_slice x3 -> x1, local copies, waits for them, and re-layouts: 25.8 us -> 1.44 us  [half_of(): lax.dynamic_index_in_dim(grad_rows.reshape(row_count, 3 * D // (2 * width...]
    reduce_scatter x1, waiting for transfers between devices: 0.01 us -> 22.8 us  [local(): merged = lax.psum_scatter(merged, 'z', scatter_dimension=0, tiled=True)]
    convert_element_type x2 -> x0, local copies, waits for them, and re-layouts: 17.7 us -> none  [the longest x1 14.4 us: local(): (jnp.concatenate([upper_rows, lower_rows], axis=1) * grad_scale).astype(j...]
    all_to_all x0 -> x1, starting transfers between devices: none -> 9.45 us  [local(): lax.all_to_all(side_terms, ('y', 'z'), split_axis=1, concat_axis=1, tiled...]
    another operation x8, local copies, waits for them, and re-layouts: 19.9 us -> 28.2 us
    reduce_scatter x1, waiting for transfers between devices: 14.7 us -> 21.8 us  [local(): merged = lax.psum_scatter(merged, 'x', scatter_dimension=1, tiled=True)]
    concatenate x1 -> x4, local copies, waits for them, and re-layouts: 0.07 us -> 5.96 us  [local(): jnp.concatenate([grad_query.reshape(row_count, D), grad_keys.reshape(row_...]
  transfers between devices with their start and end apart: 7 -> 8, of which waited for: 5 -> 5; matrix products, arithmetic and copies ran while one was open for 11% -> 17% of each run, Pallas kernels for 0% -> 0%
where the time goes in v2:
time: 337 us; the launch traced here: 333 us
  waiting for transfers between devices  98.9 us (29%)
  matrix products  70 us (21%)
  local copies, waits for them, and re-layouts  65.5 us (19%)
  starting transfers between devices  39.7 us (12%)
  blocking collectives  29.1 us (9%)
  between operations  15.1 us (4%)
  other arithmetic  14.3 us (4%)
    reduce_scatter x1, waiting for transfers between devices, local(): lax.psum_scatter(merged.reshape(D, x_size, width), 'y', scatter_dimension...  30.5 us
    another operation x8, local copies, waits for them, and re-layouts  28.2 us
    reduce_scatter x1, waiting for transfers between devices, local(): merged = lax.psum_scatter(merged, 'z', scatter_dimension=0, tiled=True)  22.8 us
    reduce_scatter x1, waiting for transfers between devices, local(): merged = lax.psum_scatter(merged, 'x', scatter_dimension=1, tiled=True)  21.8 us
    all_to_all x1, waiting for transfers between devices, local(): lax.all_to_all(tokens, ('y', 'z'), split_axis=2, concat_axis=1, tiled=True)  20.3 us
    all_gather x1, blocking collectives, local(): lax.all_gather(merged.reshape(merged.shape[0], width), ('x', 'core'), axi...  15.8 us
    dot_general x1, matrix products, local(): jnp.einsum('cphfg,cgphd->cfphd', grad_scores, key_heads, preferred_elemen...  14.1 us
    psum x1, blocking collectives, local(): side_terms = lax.psum(jnp.sum(side_terms, axis=1), ('x', 'core'))  13.3 us
  transfers between devices with their start and end apart: 8, of which 5 were waited for; matrix products, arithmetic and copies ran while one was open for 17% of the time, Pallas kernels for 0%

profile of v2, /device:TPU:1, one launch (start us, length us, event | category | flops | bytes accessed | tf_op | source)
XLA Modules:
  0.0 332.6 jit_solution(10899702626873563283)
XLA Ops:
  10.1 12.0 %all-to-all-start = ((bf16[2,8,32,1024]{3,1,0,2:T(8,128)(2,1)}), bf16[2,8,32,1024]{3,1,0,2:T(8,128)(2,1)S(1)}, u32[]{:S(2)}, u32[]{:S(2)}) async-start(bf16[2,8,32,1024]{3,1,0,2:T(8,128)(2,1)} %copy.100), calls=%async_computation | async-start | bytes 2097152 | tf_op jit(solution)/shard_map/all_to_all | solution.py:60
  26.7 20.3 %all-to-all-done = bf16[2,8,32,1024]{3,1,0,2:T(8,128)(2,1)S(1)} async-done(((bf16[2,8,32,1024]{3,1,0,2:T(8,128)(2,1)}), bf16[2,8,32,1024]{3,1,0,2:T(8,128)(2,1)S(1)}, u32[]{:S(2)}, u32[]{:S(2)}) %all-to-all-start) | async-done | bytes 1048608 | tf_op jit(solution)/shard_map/all_to_all | solution.py:60
  47.0 8.5 %all-to-all-start.1 = ((bf16[2,8,32,1024]{3,1,0,2:T(8,128)(2,1)}), bf16[2,8,32,1024]{3,1,0,2:T(8,128)(2,1)}, u32[]{:S(2)}, u32[]{:S(2)}) async-start(bf16[2,8,32,1024]{3,1,0,2:T(8,128)(2,1)} %copy.109), calls=%async_computation.1 | async-start | bytes 2097152 | tf_op jit(solution)/shard_map/all_to_all | solution.py:61
  56.9 6.6 %convolution_convert_fusion = bf16[512,3072]{1,0:T(8,128)(2,1)S(1)} fusion(bf16[512,1024]{1,0:T(8,128)(2,1)S(1)} %fusion.39, bf16[1024,3072]{1,0:T(8,128)(2,1)} %param.16), kind=kOutput, calls=%fused_computation.14 | convolution fusion | flops 3222798336 | bytes 10485760 | tf_op jit(solution)/shard_map/dot_general | solution.py:77
  65.2 4.0 %reshape.327 = bf16[2,256,16,64]{3,2,1,0:T(8,128)(2,1)} reshape(bf16[512,1024]{1,0:T(8,128)(2,1)} %get-tuple-element.27) | data formatting | bytes 2097152 | tf_op jit(solution)/shard_map/reshape.2
  69.2 3.6 %copy.107 = bf16[2,256,16,64]{1,3,2,0:T(8,128)(2,1)} copy(bf16[2,256,16,64]{3,2,1,0:T(8,128)(2,1)} %reshape.327) | data formatting | bytes 2097152 | tf_op jit(solution)/shard_map/reshape.2
  72.8 4.0 %reshape.326 = bf16[2,256,16,64]{3,2,1,0:T(8,128)(2,1)} reshape(bf16[512,1024]{1,0:T(8,128)(2,1)} %get-tuple-element.28) | data formatting | bytes 2097152 | tf_op jit(solution)/shard_map/reshape.15
  76.9 3.5 %copy.115 = bf16[2,256,16,64]{1,3,2,0:T(8,128)(2,1)} copy(bf16[2,256,16,64]{3,2,1,0:T(8,128)(2,1)} %reshape.326) | data formatting | bytes 2097152 | tf_op jit(solution)/shard_map/reshape.15
  80.4 4.0 %reshape.329 = bf16[2,256,16,64]{3,2,1,0:T(8,128)(2,1)} reshape(bf16[512,1024]{1,0:T(8,128)(2,1)} %get-tuple-element.26) | data formatting | bytes 2097152 | tf_op jit(solution)/shard_map/reshape.10
  84.4 3.6 %copy.114 = bf16[2,256,16,64]{1,3,2,0:T(8,128)(2,1)} copy(bf16[2,256,16,64]{3,2,1,0:T(8,128)(2,1)} %reshape.329) | data formatting | bytes 2097152 | tf_op jit(solution)/shard_map/reshape.10
  98.0 6.2 %fusion.100 = f32[2,16,256,256]{2,3,1,0:T(8,128)} fusion(bf16[2,256,16,64]{1,3,2,0:T(8,128)(2,1)} %copy.113, bf16[2,256,16,64]{1,3,2,0:T(8,128)(2,1)} %copy.114), kind=kOutput, calls=%fused_computation.112 | convolution fusion | flops 268435456 | bytes 10485760 | tf_op jit(solution)/shard_map/cfphd,cgphd->cphfg/dot_general | solution.py:95
  104.2 5.9 %fusion.99 = (f32[2,16,256]{2,1,0:T(8,128)S(1)}, f32[2,16,256,256]{2,3,1,0:T(8,128)}) fusion(pred[2,256,256]{1,2,0:T(8,128)(4,1)S(1)} %copy.105, bf16[2,256,16,64]{1,3,2,0:T(8,128)(2,1)S(1)} %copy-done.13, bf16[2,256,16,64]{1,3,2,0:T(8,128)(2,1)S(1)} %copy-done.14), kind=kOutput, calls=%fused_computation.111 | convolution fusion | flops 549454080 | bytes 10649600 | tf_op jit(solution)/shard_map/sub | solution.py:86
  110.1 14.1 %fusion.64 = bf16[2,256,1,16,64]{1,4,3,0,2:T(8,128)(2,1)} fusion(bf16[2,256,16,64]{1,3,2,0:T(8,128)(2,1)S(1)} %copy-done.14, f32[2,16,256,256]{2,3,1,0:T(8,128)} %fusion.100, f32[2,16,256,256]{2,3,1,0:T(8,128)} %get-tuple-element.32, f32[2,16,256]{2,1,0:T(8,128)S(1)} %get-tuple-element.31), kind=kOutput, calls=%fused_computation.62 | convolution fusion | flops 283648256 | bytes 18907136 | tf_op jit(solution)/shard_map/cphfg,cgphd->cfphd/dot_general | solution.py:101
  124.2 13.2 %fusion.61 = bf16[2,256,1,16,64]{1,4,3,0,2:T(8,128)(2,1)} fusion(bf16[2,256,16,64]{1,3,2,0:T(8,128)(2,1)S(1)} %copy-done.13, f32[2,16,256,256]{2,3,1,0:T(8,128)} %fusion.100, f32[2,16,256,256]{2,3,1,0:T(8,128)} %get-tuple-element.32, f32[2,16,256]{2,1,0:T(8,128)S(1)} %get-tuple-element.31), kind=kOutput, calls=%fused_computation.61 | convolution fusion | flops 283648256 | bytes 18907136 | tf_op jit(solution)/shard_map/cphfg,cfphd->cgphd/dot_general | solution.py:104
  137.4 4.9 %fusion.70 = bf16[2,256,1,16,64]{1,4,3,0,2:T(8,128)(2,1)S(1)} fusion(bf16[2,256,16,64]{1,3,2,0:T(8,128)(2,1)S(1)} %copy-done.7, f32[2,16,256,256]{2,3,1,0:T(8,128)} %get-tuple-element.32, f32[2,16,256]{2,1,0:T(8,128)S(1)} %get-tuple-element.31), kind=kOutput, calls=%fused_computation.64 | convolution fusion | flops 273154048 | bytes 10518528 | tf_op jit(solution)/shard_map/cphfg,cfphd->cgphd/dot_general | solution.py:107
  174.1 3.4 %collective-permute-done = bf16[1024,2048]{1,0:T(8,128)(2,1)} collective-permute-done((bf16[1024,2048]{1,0:T(8,128)(2,1)}, bf16[1024,2048]{1,0:T(8,128)(2,1)}, u32[]{:S(2)}, u32[]{:S(2)}) %collective-permute-start) | collective-permute-done | bytes 4194336 | tf_op jit(solution)/shard_map/ppermute | solution.py:158
  184.9 8.1 %fusion.44 = (f32[1024]{0:T(1024)S(1)}, f32[512]{0:T(512)S(1)}, f32[512]{0:T(512)S(1)}, f32[1024]{0:T(1024)S(1)}, f32[512,1024]{1,0:T(8,128)}) fusion(f32[512]{0:T(512)S(1)} %div.35, f32[512]{0:T(512)S(1)} %rsqrt.13, bf16[2,8,32,1024]{3,1,0,2:T(8,128)(2,1)S(1)} %all-to-all-done, f32[1024]{0:T(1024)S(1)} %copy-done.19, bf16[1024,3072]{1,0:T(8,128)(2,1)} %param.16, ...), kind=kOutput, calls=%fused_computation.50 | convolution fusion | flops 3235902464 | bytes 12603392 | tf_op jit(solution)/shard_map/dot_general | solution.py:38
  193.8 9.5 %all-to-all-start.3 = ((f32[2,32,32]{2,0,1:T(2,128)}), f32[2,32,32]{2,0,1:T(2,128)S(1)}, u32[]{:S(2)}, u32[]{:S(2)}) async-start(f32[2,32,32]{2,0,1:T(2,128)} %pad_maximum_fusion), calls=%async_computation.6 | async-start | bytes 65536 | tf_op jit(solution)/shard_map/all_to_all | solution.py:139
  203.4 30.5 %reduce-scatter.4.cloned.1.call-done = bf16[256,4,512]{2,0,1:T(8,128)(2,1)} async-done(((bf16[1024,4,512]{2,0,1:T(8,128)(2,1)}), bf16[256,4,512]{2,0,1:T(8,128)(2,1)}) %reduce-scatter.4.cloned.1.call-update) | async-done | bytes 1048592 | tf_op jit(solution)/shard_map/reduce_scatter | solution.py:160
  238.2 8.2 %all-to-all-start.2 = ((bf16[2,256,1,1024]{3,0,2,1:T(2,128)(2,1)}), bf16[2,256,1,1024]{3,0,2,1:T(2,128)(2,1)}, u32[]{:S(2)}, u32[]{:S(2)}) async-start(bf16[2,256,1,1024]{3,0,2,1:T(2,128)(2,1)} %copy.124), calls=%async_computation.2 | async-start | bytes 2097152 | tf_op jit(solution)/shard_map/all_to_all | solution.py:130
  246.5 13.3 %psum.7 = f32[2,32]{1,0:T(2,128)S(1)} all-reduce(f32[2,32]{1,0:T(2,128)S(1)} %reduce_sum.89), channel_id=1, replica_groups=mesh['x'=4,'core'=2,'y'=4,'z'=8] {'x','core'}, use_global_device_ids=true, to_apply=%region_14.15 | all-reduce | flops 64 | bytes 512 | tf_op jit(solution)/shard_map/psum | solution.py:140
  260.3 22.8 %reduce-scatter.6.cloned.1.call-done = bf16[32,4,512]{2,0,1:T(8,128)(2,1)} async-done(((bf16[256,4,512]{2,0,1:T(8,128)(2,1)}), bf16[32,4,512]{2,0,1:T(8,128)(2,1)}) %reduce-scatter.6.cloned.1.call-update) | async-done | bytes 131088 | tf_op jit(solution)/shard_map/reduce_scatter | solution.py:161
  286.8 21.8 %reduce-scatter.8.cloned.1.call-done = bf16[32,1,512]{2,0,1:T(8,128)(2,1)} async-done(((bf16[32,4,512]{2,0,1:T(8,128)(2,1)}), bf16[32,1,512]{2,0,1:T(8,128)(2,1)}) %reduce-scatter.8.cloned.1.call-update) | async-done | bytes 32784 | tf_op jit(solution)/shard_map/reduce_scatter | solution.py:162
  308.5 15.8 %all-gather = bf16[32,1,4096]{2,0,1:T(8,128)(2,1)S(1)} all-gather(bf16[32,1,512]{2,0,1:T(8,128)(2,1)} %reduce-scatter.8.cloned.1.call-done), channel_id=2, replica_groups=mesh['x'=4,'core'=2,'y'=4,'z'=8] {'x','core'}, dimensions={2}, use_global_device_ids=true | all-gather | bytes 294912 | tf_op jit(solution)/shard_map/all_gather | solution.py:163
  (118 shorter events, 69.6 us)
Async XLA Ops:
  7.2 83.1 %copy-start = (bf16[1024,1024]{1,0:T(8,128)(2,1)S(1)}, bf16[1024,1024]{1,0:T(8,128)(2,1)}, u32[]{:S(2)}) copy-start(bf16[1024,1024]{1,0:T(8,128)(2,1)} %param.17) | copy-start | bytes 6291460
  7.2 15.0 %copy-start.21 = (s32[2,4,3]{1,0,2:T(2,128)S(1)}, s32[2,4,3]{1,0,2:T(2,128)}, u32[]{:S(2)}) copy-start(s32[2,4,3]{1,0,2:T(2,128)} %param.12) | copy-start | bytes 292
  7.2 15.0 %copy-start.22 = (s32[2,4]{1,0:T(2,128)S(1)}, s32[2,4]{1,0:T(2,128)}, u32[]{:S(2)}) copy-start(s32[2,4]{1,0:T(2,128)} %param.13) | copy-start | bytes 100
  10.1 36.9 %all-to-all-start = ((bf16[2,8,32,1024]{3,1,0,2:T(8,128)(2,1)}), bf16[2,8,32,1024]{3,1,0,2:T(8,128)(2,1)S(1)}, u32[]{:S(2)}, u32[]{:S(2)}) async-start(bf16[2,8,32,1024]{3,1,0,2:T(8,128)(2,1)} %copy.100), calls=%async_computation | async-start | bytes 2097152 | tf_op jit(solution)/shard_map/all_to_all | solution.py:60
  23.7 32.7 %copy-start.19 = (f32[1024]{0:T(1024)S(1)}, f32[1024]{0:T(1024)}, u32[]{:S(2)}) copy-start(f32[1024]{0:T(1024)} %param.14) | copy-start | bytes 12292
  23.7 32.7 %copy-start.20 = (f32[1024]{0:T(1024)S(1)}, f32[1024]{0:T(1024)}, u32[]{:S(2)}) copy-start(f32[1024]{0:T(1024)} %param.15) | copy-start | bytes 12292
  47.0 41.0 %all-to-all-start.1 = ((bf16[2,8,32,1024]{3,1,0,2:T(8,128)(2,1)}), bf16[2,8,32,1024]{3,1,0,2:T(8,128)(2,1)}, u32[]{:S(2)}, u32[]{:S(2)}) async-start(bf16[2,8,32,1024]{3,1,0,2:T(8,128)(2,1)} %copy.109), calls=%async_computation.1 | async-start | bytes 2097152 | tf_op jit(solution)/shard_map/all_to_all | solution.py:61
  55.5 178.4 %reduce-scatter.4.cloned.1.call-start = ((), (), s32[]{:S(2)}) async-start(), calls=%async_computation.7 | async-start | bytes 5242880 | tf_op jit(solution)/shard_map/reduce_scatter | solution.py:160
  98.0 6.2 %copy-start.13 = (bf16[2,256,16,64]{1,3,2,0:T(8,128)(2,1)S(1)}, bf16[2,256,16,64]{1,3,2,0:T(8,128)(2,1)}, u32[]{:S(2)}) copy-start(bf16[2,256,16,64]{1,3,2,0:T(8,128)(2,1)} %copy.107) | copy-start | bytes 3145732
  98.0 6.2 %copy-start.14 = (bf16[2,256,16,64]{1,3,2,0:T(8,128)(2,1)S(1)}, bf16[2,256,16,64]{1,3,2,0:T(8,128)(2,1)}, u32[]{:S(2)}) copy-start(bf16[2,256,16,64]{1,3,2,0:T(8,128)(2,1)} %copy.115) | copy-start | bytes 3145732
  124.2 13.2 %copy-start.7 = (bf16[2,256,16,64]{1,3,2,0:T(8,128)(2,1)S(1)}, bf16[2,256,16,64]{1,3,2,0:T(8,128)(2,1)}, u32[]{:S(2)}) copy-start(bf16[2,256,16,64]{1,3,2,0:T(8,128)(2,1)} %copy.113) | copy-start | bytes 3145732
  137.4 4.9 %copy-start.6 = (bf16[2,256,16,64]{1,3,2,0:T(8,128)(2,1)S(1)}, bf16[2,256,16,64]{1,3,2,0:T(8,128)(2,1)}, u32[]{:S(2)}) copy-start(bf16[2,256,16,64]{1,3,2,0:T(8,128)(2,1)} %copy.114) | copy-start | bytes 3145732
  137.4 6.1 %copy-start.23 = (f32[2,16,256,256]{2,3,1,0:T(8,128)S(1)}, f32[2,16,256,256]{2,3,1,0:T(8,128)}, u32[]{:S(2)}) copy-start(f32[2,16,256,256]{2,3,1,0:T(8,128)} %get-tuple-element.32) | copy-start | bytes 25165828
  143.5 3.0 copy-start.18
  147.6 7.3 %copy-start.2 = (bf16[2,256,1,16,64]{1,0,4,3,2:T(2,128)(2,1)}, bf16[2,256,1,16,64]{1,0,4,3,2:T(2,128)(2,1)S(1)}, u32[]{:S(2)}) copy-start(bf16[2,256,1,16,64]{1,0,4,3,2:T(2,128)(2,1)S(1)} %copy.120) | copy-start | bytes 3145732
  157.8 2.7 copy-start.5
  157.8 4.0 %copy-start.11 = (bf16[512,1,2,512]{0,3,2,1:T(8,128)(2,1)S(1)}, bf16[512,1,2,512]{0,3,2,1:T(8,128)(2,1)}, u32[]{:S(2)}) copy-start(bf16[512,1,2,512]{0,3,2,1:T(8,128)(2,1)} %concatenate.22) | copy-start | bytes 3145732
  168.9 8.6 %collective-permute-start = (bf16[1024,2048]{1,0:T(8,128)(2,1)}, bf16[1024,2048]{1,0:T(8,128)(2,1)}, u32[]{:S(2)}, u32[]{:S(2)}) collective-permute-start(bf16[1024,2048]{1,0:T(8,128)(2,1)} %fusion.3), channel_id=1, source_target_pairs={{0,32},{32,0},{1,33},{33,1},{2,34},{34,2},{3,35},{35,3},{4,36},{36... | collective-permute-start | bytes 12582920 | tf_op jit(solution)/shard_map/ppermute | solution.py:158
  193.8 44.4 %all-to-all-start.3 = ((f32[2,32,32]{2,0,1:T(2,128)}), f32[2,32,32]{2,0,1:T(2,128)S(1)}, u32[]{:S(2)}, u32[]{:S(2)}) async-start(f32[2,32,32]{2,0,1:T(2,128)} %pad_maximum_fusion), calls=%async_computation.6 | async-start | bytes 65536 | tf_op jit(solution)/shard_map/all_to_all | solution.py:139
  203.3 79.9 %reduce-scatter.6.cloned.1.call-start = ((), (), s32[]{:S(2)}) async-start(), calls=%async_computation.8 | async-start | bytes 1179648 | tf_op jit(solution)/shard_map/reduce_scatter | solution.py:161
  236.1 47.0 %copy-start.10 = (bf16[2,8,32,1024]{3,2,1,0:T(8,128)(2,1)S(1)}, bf16[2,8,32,1024]{3,2,1,0:T(8,128)(2,1)}, u32[]{:S(2)}) copy-start(bf16[2,8,32,1024]{3,2,1,0:T(8,128)(2,1)} %param.10) | copy-start | bytes 3145732
  238.2 45.0 %all-to-all-start.2 = ((bf16[2,256,1,1024]{3,0,2,1:T(2,128)(2,1)}), bf16[2,256,1,1024]{3,0,2,1:T(2,128)(2,1)}, u32[]{:S(2)}, u32[]{:S(2)}) async-start(bf16[2,256,1,1024]{3,0,2,1:T(2,128)(2,1)} %copy.124), calls=%async_computation.2 | async-start | bytes 2097152 | tf_op jit(solution)/shard_map/all_to_all | solution.py:130
  246.4 79.5 %copy-start.1 = (bf16[1024,1024]{1,0:T(8,128)(2,1)S(1)}, bf16[1024,1024]{1,0:T(8,128)(2,1)}, u32[]{:S(2)}) copy-start(bf16[1024,1024]{1,0:T(8,128)(2,1)} %param.17) | copy-start | bytes 6291460
  246.4 62.2 %reduce-scatter.8.cloned.1.call-start = ((), (), s32[]{:S(2)}) async-start(), calls=%async_computation.9 | async-start | bytes 163840 | tf_op jit(solution)/shard_map/reduce_scatter | solution.py:162
  (8 other events, 13.2 us)
Sparse Core Ops, SparseCore 0:
  183.2 50.6 reduce-scatter.3
  236.4 46.6 reduce-scatter.5
  285.6 22.8 reduce-scatter.7

commit v3 on v2

--- a/solution.py
+++ b/solution.py
@@ -74,12 +74,18 @@
     inv_std = lax.rsqrt(jnp.mean(centred * centred, axis=1, keepdims=True) + EPSILON)
     normal_hat = centred * inv_std
     normed = (normal_hat * norm_gain + norm_bias).astype(jnp.bfloat16)
-    projected = jnp.dot(normed, qkv_weight, preferred_element_type=jnp.float32).astype(jnp.bfloat16)
-    query_heads = projected[:, :D].reshape(head_shape)
-    key_heads = projected[:, D : 2 * D].reshape(head_shape)
-    value_heads = projected[:, 2 * D :].reshape(head_shape)
+    normed_rows = normed.reshape(clip_count, frame_count, patch_count, D)
+    grad_rows_in = grad_whole.reshape(clip_count, frame_count, patch_count, D)
+    projected = jnp.einsum(
+        "cfpk,kn->cpnf", normed_rows, qkv_weight, preferred_element_type=jnp.float32
+    ).astype(jnp.bfloat16)
+    head_shape = (clip_count, patch_count, 3, HEADS, HEAD_DIM, frame_count)
+    projected = projected.reshape(head_shape)
+    query_heads = projected[:, :, 0]
+    key_heads = projected[:, :, 1]
+    value_heads = projected[:, :, 2]
     scores = (
-        jnp.einsum("cfphd,cgphd->cphfg", query_heads, key_heads, preferred_element_type=jnp.float32)
+        jnp.einsum("cphdf,cphdg->cphfg", query_heads, key_heads, preferred_element_type=jnp.float32)
         * factor
     )
     row_max = jnp.max(jnp.where(allowed, scores, -1e30), axis=-1, keepdims=True)
@@ -87,35 +93,35 @@
     attn_prob = exp_scores / jnp.sum(exp_scores, axis=-1, keepdims=True)
     prob_bf = attn_prob.astype(jnp.bfloat16)
     attended = jnp.einsum(
-        "cphfg,cgphd->cfphd", prob_bf, value_heads, preferred_element_type=jnp.float32
-    ).astype(jnp.bfloat16)
-    attn_flat = attended.reshape(row_count, D)
+        "cphfg,cphdg->cphdf", prob_bf, value_heads, preferred_element_type=jnp.float32
+    ).astype(jnp.bfloat16)
     grad_flat = grad_whole.reshape(row_count, D)
-    grad_attn = times_transpose(grad_flat, out_weight).astype(jnp.bfloat16).reshape(head_shape)
+    grad_attn = (
+        jnp.einsum("cfpn,kn->cpkf", grad_rows_in, out_weight, preferred_element_type=jnp.float32)
+        .astype(jnp.bfloat16)
+        .reshape(clip_count, patch_count, HEADS, HEAD_DIM, frame_count)
+    )
     grad_prob = jnp.einsum(
-        "cfphd,cgphd->cphfg", grad_attn, value_heads, preferred_element_type=jnp.float32
+        "cphdf,cphdg->cphfg", grad_attn, value_heads, preferred_element_type=jnp.float32
     )
     grad_scores = (
         attn_prob * (grad_prob - jnp.sum(attn_prob * grad_prob, axis=-1, keepdims=True)) * factor
     ).astype(jnp.bfloat16)
     grad_query = jnp.einsum(
-        "cphfg,cgphd->cfphd", grad_scores, key_heads, preferred_element_type=jnp.float32
+        "cphfg,cphdg->cphdf", grad_scores, key_heads, preferred_element_type=jnp.float32
     ).astype(jnp.bfloat16)
     grad_keys = jnp.einsum(
-        "cphfg,cfphd->cgphd", grad_scores, query_heads, preferred_element_type=jnp.float32
+        "cphfg,cphdf->cphdg", grad_scores, query_heads, preferred_element_type=jnp.float32
     ).astype(jnp.bfloat16)
     grad_values = jnp.einsum(
-        "cphfg,cfphd->cgphd", prob_bf, grad_attn, preferred_element_type=jnp.float32
-    ).astype(jnp.bfloat16)
-    grad_rows = jnp.concatenate(
-        [
-            grad_query.reshape(row_count, D),
-            grad_keys.reshape(row_count, D),
-            grad_values.reshape(row_count, D),
-        ],
-        axis=1,
-    )
-    grad_normed = times_transpose(grad_rows, qkv_weight)
+        "cphfg,cphdf->cphdg", prob_bf, grad_attn, preferred_element_type=jnp.float32
+    ).astype(jnp.bfloat16)
+    grad_cols = jnp.stack([grad_query, grad_keys, grad_values], axis=2).reshape(
+        clip_count, patch_count, 3 * D, frame_count
+    )
+    grad_normed = jnp.einsum(
+        "cpnf,kn->cfpk", grad_cols, qkv_weight, preferred_element_type=jnp.float32
+    ).reshape(row_count, D)
     gain_term = jnp.sum(grad_normed * normal_hat, axis=0) * grad_scale
     bias_term = jnp.sum(grad_normed, axis=0) * grad_scale
     grad_hat = grad_normed * norm_gain
@@ -142,17 +148,23 @@
     width = (3 * D + D) // (2 * x_size)
     core = lax.axis_index("core")
 
+    attended_cols = attended.reshape(clip_count, patch_count, D, frame_count)
+
     def half_of(index):
         grad_part = lax.dynamic_index_in_dim(
-            grad_rows.reshape(row_count, 3 * D // (2 * width), 2, width), index, axis=2, keepdims=False
-        ).reshape(row_count, 3 * D // 2)
-        flat_part = lax.dynamic_slice_in_dim(grad_flat, index * width, width, axis=1)
-        return (
-            jnp.concatenate(
-                [contract_rows(normed, grad_part), contract_rows(attn_flat, flat_part)], axis=1
-            )
-            * grad_scale
-        ).astype(jnp.bfloat16)
+            grad_cols.reshape(clip_count, patch_count, 3 * D // (2 * width), 2, width, frame_count),
+            index,
+            axis=3,
+            keepdims=False,
+        ).reshape(clip_count, patch_count, 3 * D // 2, frame_count)
+        flat_part = lax.dynamic_slice_in_dim(grad_rows_in, index * width, width, axis=3)
+        upper = jnp.einsum(
+            "cfpk,cpnf->kn", normed_rows, grad_part, preferred_element_type=jnp.float32
+        )
+        lower = jnp.einsum(
+            "cpnf,cfpm->nm", attended_cols, flat_part, preferred_element_type=jnp.float32
+        )
+        return (jnp.concatenate([upper, lower], axis=1) * grad_scale).astype(jnp.bfloat16)
 
     mine = half_of(core)
     got = lax.ppermute(half_of(1 - core), "core", [(0, 1), (1, 0)])

time: 337 us -> 317 us (0.941); the launches traced: 333 us -> 316 us
  local copies, waits for them, and re-layouts: 65.5 us -> 27 us
  waiting for transfers between devices: 98.9 us -> 123 us
    another operation x8 -> x1, local copies, waits for them, and re-layouts: 28.2 us -> 0.22 us  [local(): jnp.stack([grad_query, grad_keys, grad_values], axis=2)]
    all_to_all x1, waiting for transfers between devices: 0.01 us -> 23.3 us  [local(): lax.all_to_all(grad_live, ('y', 'z'), split_axis=2, concat_axis=1, tiled=...]
    concatenate x4 -> x0, local copies, waits for them, and re-layouts: 5.96 us -> none  [local(): jnp.concatenate([grad_query.reshape(row_count, D), grad_keys.reshape(row_...]
    sub x1 -> x0, matrix products: 5.9 us -> none  [local(): exp_scores = jnp.where(allowed, jnp.exp(scores - row_max), 0.0)]
    all_to_all x1, starting transfers between devices: 9.45 us -> 4.67 us  [local(): lax.all_to_all(side_terms, ('y', 'z'), split_axis=1, concat_axis=1, tiled...]
    sub x0 -> x1, other arithmetic: none -> 3.58 us  [local(): exp_scores = jnp.where(allowed, jnp.exp(scores - row_max), 0.0)]
    dot_general x12 -> x13, matrix products: 63.6 us -> 66.5 us  [the longest x1 14.7 us: local(): jnp.einsum('cphfg,cphdg->cphdf', grad_scores, key_heads, preferred_elemen...]
    convert_element_type x4 -> x3, local copies, waits for them, and re-layouts: 6.67 us -> 8.17 us  [the longest x1 4.65 us: local(): projected = jnp.einsum('cfpk,kn->cpnf', normed_rows, qkv_weight, preferre...]
  transfers between devices with their start and end apart: 8 -> 8, of which waited for: 5 -> 6; matrix products, arithmetic and copies ran while one was open for 17% -> 7% of each run, Pallas kernels for 0% -> 0%
where the time goes in v3:
time: 317 us; the launch traced here: 316 us
  waiting for transfers between devices  123 us (39%)
  matrix products  67 us (21%)
  starting transfers between devices  38 us (12%)
  blocking collectives  29 us (9%)
  local copies, waits for them, and re-layouts  27 us (9%)
  other arithmetic  17.4 us (5%)
  between operations  14.8 us (5%)
    reduce_scatter x1, waiting for transfers between devices, local(): lax.psum_scatter(merged.reshape(D, x_size, width), 'y', scatter_dimension...  30.6 us
    reduce_scatter x1, waiting for transfers between devices, local(): merged = lax.psum_scatter(merged, 'z', scatter_dimension=0, tiled=True)  23.9 us
    all_to_all x1, waiting for transfers between devices, local(): lax.all_to_all(grad_live, ('y', 'z'), split_axis=2, concat_axis=1, tiled=...  23.3 us
    all_to_all x1, waiting for transfers between devices, local(): lax.all_to_all(tokens, ('y', 'z'), split_axis=2, concat_axis=1, tiled=True)  21.3 us
    reduce_scatter x1, waiting for transfers between devices, local(): merged = lax.psum_scatter(merged, 'x', scatter_dimension=1, tiled=True)  21.2 us
    all_gather x1, blocking collectives, local(): lax.all_gather(merged.reshape(merged.shape[0], width), ('x', 'core'), axi...  15.8 us
    dot_general x1, matrix products, local(): jnp.einsum('cphfg,cphdg->cphdf', grad_scores, key_heads, preferred_elemen...  14.7 us
    dot_general x1, matrix products, local(): jnp.einsum('cphfg,cphdf->cphdg', grad_scores, query_heads, preferred_elem...  13.8 us
  transfers between devices with their start and end apart: 8, of which 6 were waited for; matrix products, arithmetic and copies ran while one was open for 7% of the time, Pallas kernels for 0%

profile of v3, /device:TPU:1, one launch (start us, length us, event | category | flops | bytes accessed | tf_op | source)
XLA Modules:
  0.0 316.1 jit_solution(15577857029816075896)
XLA Ops:
  7.2 2.9 copy.119
  10.1 12.0 %all-to-all-start = ((bf16[2,8,32,1024]{3,1,0,2:T(8,128)(2,1)}), bf16[2,8,32,1024]{3,1,0,2:T(8,128)(2,1)S(1)}, u32[]{:S(2)}, u32[]{:S(2)}) async-start(bf16[2,8,32,1024]{3,1,0,2:T(8,128)(2,1)} %copy.119), calls=%async_computation | async-start | bytes 2097152 | tf_op jit(solution)/shard_map/all_to_all | solution.py:60
  25.8 21.3 %all-to-all-done = bf16[2,8,32,1024]{3,1,0,2:T(8,128)(2,1)S(1)} async-done(((bf16[2,8,32,1024]{3,1,0,2:T(8,128)(2,1)}), bf16[2,8,32,1024]{3,1,0,2:T(8,128)(2,1)S(1)}, u32[]{:S(2)}, u32[]{:S(2)}) %all-to-all-start) | async-done | bytes 1048608 | tf_op jit(solution)/shard_map/all_to_all | solution.py:60
  47.0 8.5 %all-to-all-start.1 = ((bf16[2,8,32,1024]{3,1,0,2:T(8,128)(2,1)}), bf16[2,8,32,1024]{3,1,0,2:T(8,128)(2,1)}, u32[]{:S(2)}, u32[]{:S(2)}) async-start(bf16[2,8,32,1024]{3,1,0,2:T(8,128)(2,1)} %copy.127), calls=%async_computation.1 | async-start | bytes 2097152 | tf_op jit(solution)/shard_map/all_to_all | solution.py:61
  57.3 23.3 %all-to-all-done.1 = bf16[2,8,32,1024]{3,1,0,2:T(8,128)(2,1)} async-done(((bf16[2,8,32,1024]{3,1,0,2:T(8,128)(2,1)}), bf16[2,8,32,1024]{3,1,0,2:T(8,128)(2,1)}, u32[]{:S(2)}, u32[]{:S(2)}) %all-to-all-start.1) | async-done | bytes 1048608 | tf_op jit(solution)/shard_map/all_to_all | solution.py:61
  80.6 3.5 %fusion.76 = bf16[2,1,1024,256]{2,3,0,1:T(8,128)(2,1)} fusion(bf16[1024,1024]{1,0:T(8,128)(2,1)S(1)} %copy-done, bf16[2,8,32,1024]{3,1,0,2:T(8,128)(2,1)} %all-to-all-done.1), kind=kOutput, calls=%fused_computation.74 | convolution fusion | flops 1074266112 | bytes 4194304 | tf_op jit(solution)/shard_map/cfpn,kn->cpkf/dot_general | solution.py:100
  85.6 7.8 %fusion.27 = bf16[2,1,3072,256]{2,3,0,1:T(8,128)(2,1)} fusion(bf16[1024,3072]{1,0:T(8,128)(2,1)} %param.16, f32[1024]{0:T(1024)S(1)} %copy-done.13, f32[1024]{0:T(1024)S(1)} %copy-done.10, f32[2,256]{1,0:T(2,128)S(1)} %rsqrt.13, f32[2,256]{1,0:T(2,128)S(1)} %div.35, bf16[2,8,32,1024]{3,1,0,2:T(8,128)(2,1)S(1)} %all-to-all-done), kind=kOutput, calls=%fused_computation.28 | convolution fusion | flops 3225944064 | bytes 10498048 | tf_op jit(solution)/shard_map/cfpk,kn->cpnf/dot_general | solution.py:79
  93.4 4.6 %copy.121 = bf16[2,1,3072,256]{3,2,0,1:T(8,128)(2,1)} copy(bf16[2,1,3072,256]{2,3,0,1:T(8,128)(2,1)} %fusion.27) | data formatting | bytes 6291456 | tf_op jit(solution)/shard_map/convert_element_type | solution.py:81
  100.9 5.7 %fusion.91 = f32[2,16,256,256]{2,3,1,0:T(8,128)} fusion(bf16[2,16,64,256]{3,2,1,0:T(8,128)(2,1)S(1)} %bitcast.220, bf16[2,1,3,16,64,256]{5,4,3,2,0,1:T(8,128)(2,1)} %bitcast.216), kind=kOutput, calls=%fused_computation.90 | convolution fusion | flops 268435456 | bytes 10485760 | tf_op jit(solution)/shard_map/cphdf,cphdg->cphfg/dot_general | solution.py:104
  106.6 3.6 %fusion.117 = (f32[2,16,256]{2,1,0:T(8,128)S(1)}, f32[2,16,256,256]{2,3,1,0:T(8,128)S(1)}) fusion(f32[2,16,256,256]{2,3,1,0:T(8,128)S(1)} %fusion.90, pred[2,256,256]{1,2,0:T(8,128)(4,1)S(1)} %copy.125), kind=kOutput, calls=%fused_computation.132 | output fusion | flops 12583167 | bytes 16941056 | tf_op jit(solution)/shard_map/sub | solution.py:92
  110.2 3.2 %copy-done.16 = f32[2,16,256,256]{2,3,1,0:T(8,128)} copy-done((f32[2,16,256,256]{2,3,1,0:T(8,128)}, f32[2,16,256,256]{2,3,1,0:T(8,128)S(1)}, u32[]{:S(2)}) %copy-start.16) | copy-done | bytes 8388632
  114.9 13.8 %fusion.73 = bf16[2,16,64,256]{3,2,1,0:T(8,128)(2,1)S(1)} fusion(f32[2,16,256,256]{2,3,1,0:T(8,128)} %fusion.91, bf16[2,1,3,16,64,256]{5,4,3,2,0,1:T(8,128)(2,1)} %bitcast.217, f32[2,16,256,256]{2,3,1,0:T(8,128)} %copy-done.16, f32[2,16,256]{2,1,0:T(8,128)S(1)} %get-tuple-element.32), kind=kOutput, calls=%fused_computation.73 | convolution fusion | flops 283648256 | bytes 35717120 | tf_op jit(solution)/shard_map/cphfg,cphdf->cphdg/dot_general | solution.py:113
  128.7 14.7 %fusion.70 = bf16[2,16,64,256]{3,2,1,0:T(8,128)(2,1)} fusion(f32[2,16,256,256]{2,3,1,0:T(8,128)} %fusion.91, bf16[2,1,3,16,64,256]{5,4,3,2,0,1:T(8,128)(2,1)} %bitcast.218, f32[2,16,256,256]{2,3,1,0:T(8,128)} %copy-done.16, f32[2,16,256]{2,1,0:T(8,128)S(1)} %get-tuple-element.32), kind=kOutput, calls=%fused_computation.72 | convolution fusion | flops 283648256 | bytes 35717120 | tf_op jit(solution)/shard_map/cphfg,cphdg->cphdf/dot_general | solution.py:110
  143.5 4.6 %fusion.64 = bf16[2,16,64,256]{3,2,1,0:T(8,128)(2,1)S(1)} fusion(bf16[2,1,3,16,64,256]{5,4,3,2,0,1:T(8,128)(2,1)} %bitcast.219, f32[2,16,256,256]{2,3,1,0:T(8,128)} %copy-done.16, f32[2,16,256]{2,1,0:T(8,128)S(1)} %get-tuple-element.32), kind=kOutput, calls=%fused_computation.70 | convolution fusion | flops 273154048 | bytes 10518528 | tf_op jit(solution)/shard_map/cphfg,cphdg->cphdf/dot_general | solution.py:95
  155.7 4.6 %collective-permute-start = (bf16[1024,2048]{1,0:T(8,128)(2,1)}, bf16[1024,2048]{1,0:T(8,128)(2,1)}, u32[]{:S(2)}, u32[]{:S(2)}) collective-permute-start(bf16[1024,2048]{1,0:T(8,128)(2,1)} %fusion.3), channel_id=1, source_target_pairs={{0,32},{32,0},{1,33},{33,1},{2,34},{34,2},{3,35},{35,3},{4,36},{36... | collective-permute-start | bytes 12582920 | tf_op jit(solution)/shard_map/ppermute | solution.py:170
  167.4 3.1 add_convert_fusion
  176.1 6.4 %fusion.52 = (f32[1024]{0:T(1024)S(1)}, f32[2,256]{1,0:T(2,128)S(1)}, f32[2,256]{1,0:T(2,128)S(1)}, f32[2,256,1024]{2,1,0:T(8,128)S(1)}) fusion(f32[2,256]{1,0:T(2,128)S(1)} %div.35, f32[2,256]{1,0:T(2,128)S(1)} %rsqrt.13, bf16[2,8,32,1024]{3,1,0,2:T(8,128)(2,1)S(1)} %all-to-all-done, f32[1024]{0:T(1024)S(1)} %copy-done.10, ...), kind=kOutput, calls=%fused_computation.56 | convolution fusion | flops 3225942016 | bytes 12599296 | tf_op jit(solution)/shard_map/cpnf,kn->cfpk/dot_general | solution.py:122
  183.5 4.7 %all-to-all-start.3 = ((f32[2,32,32]{2,0,1:T(2,128)}), f32[2,32,32]{2,0,1:T(2,128)S(1)}, u32[]{:S(2)}, u32[]{:S(2)}) async-start(f32[2,32,32]{2,0,1:T(2,128)} %pad_maximum_fusion.2), calls=%async_computation.6 | async-start | bytes 65536 | tf_op jit(solution)/shard_map/all_to_all | solution.py:145
  188.2 30.6 %reduce-scatter.4.cloned.1.call-done = bf16[256,4,512]{2,0,1:T(8,128)(2,1)} async-done(((bf16[1024,4,512]{2,0,1:T(8,128)(2,1)}), bf16[256,4,512]{2,0,1:T(8,128)(2,1)}) %reduce-scatter.4.cloned.1.call-update) | async-done | bytes 1048592 | tf_op jit(solution)/shard_map/reduce_scatter | solution.py:172
  221.5 8.1 %all-to-all-start.2 = ((bf16[2,256,1,1024]{3,0,2,1:T(2,128)(2,1)}), bf16[2,256,1,1024]{3,0,2,1:T(2,128)(2,1)}, u32[]{:S(2)}, u32[]{:S(2)}) async-start(bf16[2,256,1,1024]{3,0,2,1:T(2,128)(2,1)} %copy.136), calls=%async_computation.2 | async-start | bytes 2097152 | tf_op jit(solution)/shard_map/all_to_all | solution.py:136
  229.8 13.2 %psum.7 = f32[2,32]{1,0:T(2,128)S(1)} all-reduce(f32[2,32]{1,0:T(2,128)S(1)} %reduce_sum.89), channel_id=1, replica_groups=mesh['x'=4,'core'=2,'y'=4,'z'=8] {'x','core'}, use_global_device_ids=true, to_apply=%region_14.15 | all-reduce | flops 64 | bytes 512 | tf_op jit(solution)/shard_map/psum | solution.py:146
  243.5 23.9 %reduce-scatter.6.cloned.1.call-done = bf16[32,4,512]{2,0,1:T(8,128)(2,1)} async-done(((bf16[256,4,512]{2,0,1:T(8,128)(2,1)}), bf16[32,4,512]{2,0,1:T(8,128)(2,1)}) %reduce-scatter.6.cloned.1.call-update) | async-done | bytes 131088 | tf_op jit(solution)/shard_map/reduce_scatter | solution.py:173
  271.1 21.2 %reduce-scatter.8.cloned.1.call-done = bf16[32,1,512]{2,0,1:T(8,128)(2,1)} async-done(((bf16[32,4,512]{2,0,1:T(8,128)(2,1)}), bf16[32,1,512]{2,0,1:T(8,128)(2,1)}) %reduce-scatter.8.cloned.1.call-update) | async-done | bytes 32784 | tf_op jit(solution)/shard_map/reduce_scatter | solution.py:174
  292.3 15.8 %all-gather = bf16[32,1,4096]{2,0,1:T(8,128)(2,1)S(1)} all-gather(bf16[32,1,512]{2,0,1:T(8,128)(2,1)} %reduce-scatter.8.cloned.1.call-done), channel_id=2, replica_groups=mesh['x'=4,'core'=2,'y'=4,'z'=8] {'x','core'}, dimensions={2}, use_global_device_ids=true | all-gather | bytes 294912 | tf_op jit(solution)/shard_map/all_gather | solution.py:175
  (89 shorter events, 40.3 us)
Async XLA Ops:
  7.2 73.5 %copy-start = (bf16[1024,1024]{1,0:T(8,128)(2,1)S(1)}, bf16[1024,1024]{1,0:T(8,128)(2,1)}, u32[]{:S(2)}) copy-start(bf16[1024,1024]{1,0:T(8,128)(2,1)} %param.17) | copy-start | bytes 6291460
  10.1 36.9 %all-to-all-start = ((bf16[2,8,32,1024]{3,1,0,2:T(8,128)(2,1)}), bf16[2,8,32,1024]{3,1,0,2:T(8,128)(2,1)S(1)}, u32[]{:S(2)}, u32[]{:S(2)}) async-start(bf16[2,8,32,1024]{3,1,0,2:T(8,128)(2,1)} %copy.119), calls=%async_computation | async-start | bytes 2097152 | tf_op jit(solution)/shard_map/all_to_all | solution.py:60
  22.8 32.7 %copy-start.11 = (s32[2,4,3]{1,0,2:T(2,128)S(1)}, s32[2,4,3]{1,0,2:T(2,128)}, u32[]{:S(2)}) copy-start(s32[2,4,3]{1,0,2:T(2,128)} %param.12) | copy-start | bytes 292
  22.8 32.8 %copy-start.12 = (s32[2,4]{1,0:T(2,128)S(1)}, s32[2,4]{1,0:T(2,128)}, u32[]{:S(2)}) copy-start(s32[2,4]{1,0:T(2,128)} %param.13) | copy-start | bytes 100
  47.0 33.6 %all-to-all-start.1 = ((bf16[2,8,32,1024]{3,1,0,2:T(8,128)(2,1)}), bf16[2,8,32,1024]{3,1,0,2:T(8,128)(2,1)}, u32[]{:S(2)}, u32[]{:S(2)}) async-start(bf16[2,8,32,1024]{3,1,0,2:T(8,128)(2,1)} %copy.127), calls=%async_computation.1 | async-start | bytes 2097152 | tf_op jit(solution)/shard_map/all_to_all | solution.py:61
  55.5 163.3 %reduce-scatter.4.cloned.1.call-start = ((), (), s32[]{:S(2)}) async-start(), calls=%async_computation.7 | async-start | bytes 5242880 | tf_op jit(solution)/shard_map/reduce_scatter | solution.py:172
  57.3 28.3 %copy-start.10 = (f32[1024]{0:T(1024)S(1)}, f32[1024]{0:T(1024)}, u32[]{:S(2)}) copy-start(f32[1024]{0:T(1024)} %param.14) | copy-start | bytes 12292
  57.3 28.3 %copy-start.13 = (f32[1024]{0:T(1024)S(1)}, f32[1024]{0:T(1024)}, u32[]{:S(2)}) copy-start(f32[1024]{0:T(1024)} %param.15) | copy-start | bytes 12292
  110.2 3.2 %copy-start.16 = (f32[2,16,256,256]{2,3,1,0:T(8,128)}, f32[2,16,256,256]{2,3,1,0:T(8,128)S(1)}, u32[]{:S(2)}) copy-start(f32[2,16,256,256]{2,3,1,0:T(8,128)S(1)} %get-tuple-element.33) | copy-start | bytes 25165828
  114.9 33.2 %copy-start.3 = (bf16[2,16,64,256]{3,2,1,0:T(8,128)(2,1)}, bf16[2,16,64,256]{3,2,1,0:T(8,128)(2,1)S(1)}, u32[]{:S(2)}) copy-start(bf16[2,16,64,256]{3,2,1,0:T(8,128)(2,1)S(1)} %fusion.61) | copy-start | bytes 3145732
  128.7 19.4 %copy-start.5 = (bf16[2,16,64,256]{3,2,1,0:T(8,128)(2,1)}, bf16[2,16,64,256]{3,2,1,0:T(8,128)(2,1)S(1)}, u32[]{:S(2)}) copy-start(bf16[2,16,64,256]{3,2,1,0:T(8,128)(2,1)S(1)} %fusion.73) | copy-start | bytes 3145732
  143.5 4.7 %copy-start.7 = (bf16[2,16,64,256]{3,2,1,0:T(8,128)(2,1)S(1)}, bf16[2,16,64,256]{3,2,1,0:T(8,128)(2,1)}, u32[]{:S(2)}) copy-start(bf16[2,16,64,256]{3,2,1,0:T(8,128)(2,1)} %fusion.70) | copy-start | bytes 3145732
  148.1 2.1 copy-start.14
  155.7 11.7 %collective-permute-start = (bf16[1024,2048]{1,0:T(8,128)(2,1)}, bf16[1024,2048]{1,0:T(8,128)(2,1)}, u32[]{:S(2)}, u32[]{:S(2)}) collective-permute-start(bf16[1024,2048]{1,0:T(8,128)(2,1)} %fusion.3), channel_id=1, source_target_pairs={{0,32},{32,0},{1,33},{33,1},{2,34},{34,2},{3,35},{35,3},{4,36},{36... | collective-permute-start | bytes 12582920 | tf_op jit(solution)/shard_map/ppermute | solution.py:170
  160.3 1.2 copy-start.9
  160.3 1.5 copy-start.15
  172.7 1.2 copy-start.4
  172.7 1.5 copy-start.6
  183.5 38.1 %all-to-all-start.3 = ((f32[2,32,32]{2,0,1:T(2,128)}), f32[2,32,32]{2,0,1:T(2,128)S(1)}, u32[]{:S(2)}, u32[]{:S(2)}) async-start(f32[2,32,32]{2,0,1:T(2,128)} %pad_maximum_fusion.2), calls=%async_computation.6 | async-start | bytes 65536 | tf_op jit(solution)/shard_map/all_to_all | solution.py:145
  188.1 79.2 %reduce-scatter.6.cloned.1.call-start = ((), (), s32[]{:S(2)}) async-start(), calls=%async_computation.8 | async-start | bytes 1179648 | tf_op jit(solution)/shard_map/reduce_scatter | solution.py:173
  219.4 47.9 %copy-start.2 = (bf16[2,8,32,1024]{3,2,1,0:T(8,128)(2,1)S(1)}, bf16[2,8,32,1024]{3,2,1,0:T(8,128)(2,1)}, u32[]{:S(2)}) copy-start(bf16[2,8,32,1024]{3,2,1,0:T(8,128)(2,1)} %param.10) | copy-start | bytes 3145732
  221.5 45.9 %all-to-all-start.2 = ((bf16[2,256,1,1024]{3,0,2,1:T(2,128)(2,1)}), bf16[2,256,1,1024]{3,0,2,1:T(2,128)(2,1)}, u32[]{:S(2)}, u32[]{:S(2)}) async-start(bf16[2,256,1,1024]{3,0,2,1:T(2,128)(2,1)} %copy.136), calls=%async_computation.2 | async-start | bytes 2097152 | tf_op jit(solution)/shard_map/all_to_all | solution.py:136
  229.7 62.6 %reduce-scatter.8.cloned.1.call-start = ((), (), s32[]{:S(2)}) async-start(), calls=%async_computation.9 | async-start | bytes 163840 | tf_op jit(solution)/shard_map/reduce_scatter | solution.py:174
  267.4 42.2 %copy-start.1 = (bf16[1024,1024]{1,0:T(8,128)(2,1)S(1)}, bf16[1024,1024]{1,0:T(8,128)(2,1)}, u32[]{:S(2)}) copy-start(bf16[1024,1024]{1,0:T(8,128)(2,1)} %param.17) | copy-start | bytes 6291460
  (1 other events, 1.0 us)
Sparse Core Ops, SparseCore 0:
  172.9 45.8 reduce-scatter.3
  221.3 46.0 reduce-scatter.5
  269.8 22.3 reduce-scatter.7
